TPU v7x, 128 devices: a whole 4x4x4 slice. The times are simulated.
128 devices in a mesh: row: 8 (over z, core), col: 16 (over y, x).
Axes of the slice: x: 4, y: 4, z: 4, core: 2. Of those that a mesh axis runs over, the one named last changes fastest.
Arguments:
- coeffs: float32 [2048, 3, 64, 128], P(('row', 'col')), may hold values from -0.18 to 0.18
- degree: int32 [2048], P(('row', 'col')), may hold values from 16 to 63
- material: float32 [2048, 2], P(('row', 'col')), may hold values from 0.2 to 2
- split_coeffs: float32 [512, 3, 64, 64], P(('row', 'col')), may hold values from -0.18 to 0.18
- split_material: float32 [256, 2], replicated, may hold values from 0.2 to 2
- separation: float32 [3, 2048, 8], P(None, ('row', 'col')), may hold values from -2.6 to 2.6, as said below
- reader_dev: int32 [2048, 8], P(('row', 'col')), may hold values from 0 to 127, all different within a row; in each aligned block of 16 rows (0 to 15, 16 to 31, ...) at most 2 rows name the same one
- reader_slot: int32 [2048, 8], P(('row', 'col')), may hold values from 0 to 15
Outputs:
- traction_coeffs: float32 [2048, 64, 128], P(('row', 'col'))
- split_traction: float32 [512, 64, 64], P(('row', 'col'))
- near_velocity: float32 [3, 8192], P(None, ('row', 'col'))
Inputs may be any that keep to these rules, and one draw needn't show every extreme that they name: `reader_dev`: each ordinary drop names 8 different devices; among the drops of one device at most 2 name the same device, and some device is named exactly 2 times. Each entry's separation vector has a length between 1.9 and 2.6.
All inputs are finite; a program needn't handle non-finite values.
Results may differ from a plain program's by a relative error of at most 0.019.
Values may be sent and summed in bfloat16 or wider, within the bound.
No kernel may reach another device: no remote copies, remote signals or barrier semaphores. Data moves between devices by JAX's collectives and lax.ppermute only.
A program may use at most 128 MiB of HBM per device.

v0:
```python
import math

import jax
import jax.numpy as jnp
import numpy as np
from jax import lax
from jax.experimental import pallas as pl
from jax.experimental.pallas import tpu as pltpu
from jax.sharding import PartitionSpec as P

HIGH = lax.Precision.HIGHEST
SOFTENING = 0.04


def from_partner(block, axis, stride):
    count = lax.axis_size(axis)
    route = []
    for low in range(count):
        high = low | 1 << stride
        if high != low and high < count:
            route += [(low, high), (high, low)]
    return lax.ppermute(block, axis, route)


def spectral_tables(degrees):
    nlon = 2 * degrees
    theta_lat = (np.arange(degrees) + 0.5) * (math.pi / degrees)
    cosine = np.cos(theta_lat)
    sine_theta = np.sin(theta_lat)
    legendre = np.zeros((degrees, degrees, degrees))
    for order in range(degrees):
        log_total = 0.0
        for step_index in range(1, order + 1):
            log_total = log_total + math.log((2.0 * step_index + 1.0) / (2.0 * step_index))
        diag_value = np.exp(0.5 * log_total + order * np.log(sine_theta)) / math.sqrt(4.0 * math.pi)
        legendre[order, :, order] = diag_value
        prev_two = diag_value
        if order + 1 < degrees:
            prev_one = math.sqrt(2.0 * order + 3.0) * cosine * diag_value
            legendre[order, :, order + 1] = prev_one
            for level in range(order + 2, degrees):
                alpha_term = math.sqrt(
                    (4.0 * level * level - 1.0) / (level * level - order * order)
                )
                beta_term = math.sqrt(
                    ((level - 1.0) ** 2 - order * order) / (4.0 * (level - 1.0) ** 2 - 1.0)
                )
                current = alpha_term * (cosine * prev_one - beta_term * prev_two)
                legendre[order, :, level] = current
                prev_two = prev_one
                prev_one = current
    order_index = np.arange(degrees)
    lon_index = np.arange(nlon)
    phase_angle = order_index[:, None] * lon_index[None, :] % nlon * (2.0 * math.pi / nlon)
    fourier = np.concatenate([np.cos(phase_angle), np.sin(phase_angle)], axis=0)
    quad_weight = sine_theta * (math.pi / degrees) * (2.0 * math.pi / nlon)
    longitude = lon_index * (2.0 * math.pi / nlon)
    normals = np.stack(
        [
            sine_theta[:, None] * np.cos(longitude)[None, :],
            sine_theta[:, None] * np.sin(longitude)[None, :],
            cosine[:, None] * np.ones((1, nlon)),
        ],
        axis=0,
    )
    return (
        jnp.asarray(legendre, dtype=jnp.float32),
        jnp.asarray(fourier, dtype=jnp.float32),
        jnp.asarray(quad_weight, dtype=jnp.float32),
        jnp.asarray(normals, dtype=jnp.float32),
    )


def legendre_synth(coeff, legendre):
    batch_size, degrees, coef_width = coeff.shape
    orders = legendre.shape[0]
    parted = coeff.reshape(batch_size, degrees, 2, orders)
    return jnp.einsum("mjl,nlcm->njcm", legendre, parted, precision=HIGH)


def fourier_synth(partial_legendre, fourier_rows):
    batch_size, nlat, two, orders = partial_legendre.shape
    return jnp.einsum(
        "njw,wk->njk",
        partial_legendre.reshape(batch_size, nlat, two * orders),
        fourier_rows,
        precision=HIGH,
    )


def analysis_fourier(traction_grid, fourier, quad_weight):
    batch_size, nlat, nlon = traction_grid.shape
    projected = (
        jnp.einsum("bjk,wk->bjw", traction_grid, fourier, precision=HIGH)
        * quad_weight[None, :, None]
    )
    return projected.reshape(batch_size, nlat, 2, fourier.shape[0] // 2)


def analysis_legendre(coef_grid, legendre):
    batch_size = coef_grid.shape[0]
    result = jnp.einsum("mjl,bjcm->blcm", legendre, coef_grid, precision=HIGH)
    return result.reshape(batch_size, legendre.shape[2], 2 * legendre.shape[0])


def prepare(coeffs, keep_mask):
    degrees = coeffs.shape[2]
    degree_value = jnp.arange(degrees, dtype=jnp.float32)
    shape_part = coeffs[:, 0] * keep_mask
    curvature = (
        shape_part * (degree_value * (degree_value + 1.0) / (degrees * degrees))[None, :, None]
    )
    electric = 3.0 * coeffs[:, 1] * keep_mask
    viscous = 3.0 * coeffs[:, 2] * keep_mask * ((degree_value + 2.0) / degrees)[None, :, None]
    return jnp.stack([shape_part, curvature, electric, viscous], axis=1)


def traction(surface, material):
    radius = jnp.exp(surface[:, 0])
    traction_grid = (
        material[:, 0, None, None] * surface[:, 1]
        + 0.5 * surface[:, 2] * surface[:, 2]
        + 2.0 * material[:, 1, None, None] * surface[:, 3]
    )
    return (radius, traction_grid)


def velocity_terms(
    radius, traction_grid, spacing, target_radius, cell_weight, cell_normal, target_normal
):
    load_grid = traction_grid * radius * radius * cell_weight[None, :]
    target_point = spacing[:, :, None] + target_radius[None] * target_normal[:, None, :]
    surface_point = radius[None] * cell_normal[:, None, :]
    offset = target_point[:, :, :, None] - surface_point[:, :, None, :]
    distance_sq = jnp.sum(offset * offset, axis=0)
    softened = distance_sq + SOFTENING
    weight = load_grid[:, None, :] / (softened * jnp.sqrt(softened))
    normal_dot = jnp.sum(offset * cell_normal[:, None, None, :], axis=0)
    stokeslet = weight[None] * (
        cell_normal[:, None, None, :] * (distance_sq + 2.0 * SOFTENING)[None]
        + offset * normal_dot[None]
    )
    return jnp.sum(stokeslet, axis=3) / (8.0 * math.pi)


def per_device(
    coeffs, degree, material, split_coeffs, split_material, separation, reader_dev, reader_slot
):
    drop_count, fields, degrees, coef_width = coeffs.shape
    legendre, fourier, quad_weight, normals = spectral_tables(degrees)
    nlat = legendre.shape[1]
    nlon = fourier.shape[1]
    degree_index = jnp.arange(degrees, dtype=jnp.int32)
    order_full = jnp.arange(coef_width, dtype=jnp.int32) % degrees
    order_mask = (degree_index[:, None] >= order_full[None, :]).astype(jnp.float32)
    keep_mask = order_mask[None] * (degree_index[None, :, None] <= degree[:, None, None]).astype(
        jnp.float32
    )
    prepared = prepare(coeffs, keep_mask)
    partial_legendre = legendre_synth(
        prepared.reshape(drop_count * 4, degrees, coef_width), legendre
    )
    surface = fourier_synth(partial_legendre, fourier).reshape(drop_count, 4, nlat, nlon)
    radius, traction_grid = traction(surface, material)
    traction_coeffs = (
        analysis_legendre(analysis_fourier(traction_grid, fourier, quad_weight), legendre)
        * keep_mask
    )
    split_count = split_coeffs.shape[0]
    half_width = split_coeffs.shape[3]
    half_orders = half_width // 2
    half_index = lax.axis_index("row") % 2
    pair_start = (
        lax.axis_index("row") // 2 * lax.axis_size("col") + lax.axis_index("col")
    ) * split_count
    own_material = lax.dynamic_slice_in_dim(split_material, pair_start, split_count, 0)
    own_order = half_index * half_orders + jnp.arange(half_width, dtype=jnp.int32) % half_orders
    keep_half = (degree_index[:, None] >= own_order[None, :]).astype(jnp.float32)
    own_legendre = lax.dynamic_slice_in_dim(legendre, half_index * half_orders, half_orders, 0)
    own_fourier = lax.dynamic_slice_in_dim(
        fourier.reshape(2, degrees, nlon), half_index * half_orders, half_orders, 1
    ).reshape(half_width, nlon)
    split_prepared = prepare(split_coeffs, keep_half[None])
    split_legendre = legendre_synth(
        split_prepared.reshape(split_count * 4, degrees, half_width), own_legendre
    )
    partial_surface = fourier_synth(split_legendre, own_fourier)
    split_surface = partial_surface + from_partner(
        partial_surface.astype(jnp.bfloat16), "row", 0
    ).astype(partial_surface.dtype)
    split_radius, split_grid = traction(
        split_surface.reshape(split_count, 4, nlat, nlon), own_material
    )
    coef_grid = analysis_fourier(split_grid, fourier, quad_weight)
    own_grid = lax.dynamic_slice_in_dim(coef_grid, half_index * half_orders, half_orders, 3)
    split_traction = analysis_legendre(own_grid, own_legendre) * keep_half[None]
    near_grid = jnp.stack([radius, traction_grid], axis=1).astype(jnp.bfloat16)
    point_grid = near_grid[:, 0, nlat // 4 :: nlat // 2, :: nlon // 2]
    point_count = point_grid.shape[1] * point_grid.shape[2]
    own_points = point_grid.reshape(drop_count, point_count)
    target_normal = normals[:, nlat // 4 :: nlat // 2, :: nlon // 2].reshape(3, point_count)
    all_points = lax.all_gather(own_points, ("row", "col"), axis=0, tiled=True)
    total_drops = all_points.shape[0]
    readers = reader_dev.shape[1]
    target = (reader_dev * drop_count + reader_slot).reshape(-1)
    pick = (target[:, None] == jnp.arange(total_drops, dtype=jnp.int32)[None, :]).astype(
        jnp.float32
    )
    target_radius = jnp.dot(pick, all_points.astype(jnp.float32), precision=HIGH)
    target_point = separation.reshape(3, drop_count * readers)[:, :, None] + (
        target_radius[None] * target_normal[:, None, :]
    )
    target_point = jnp.transpose(
        target_point.reshape(3, drop_count, readers * point_count), (1, 2, 0)
    ).reshape(-1)
    source_radius = near_grid[:, 0].astype(jnp.float32)
    source_traction = near_grid[:, 1].astype(jnp.float32)
    cell_weight = jnp.broadcast_to(quad_weight[:, None], (nlat, nlon))
    partial = near_field(target_point, source_radius, source_traction, normals, cell_weight)
    contribution = jnp.sum(partial, axis=3) / (8.0 * math.pi)
    contribution = jnp.transpose(
        contribution.reshape(drop_count, 3, readers, point_count), (0, 2, 1, 3)
    ).reshape(drop_count * readers, 3 * point_count)
    dense = jnp.dot(jnp.transpose(pick), contribution, precision=HIGH)
    mine = lax.psum_scatter(dense, ("row", "col"), scatter_dimension=0, tiled=True)
    near_velocity = jnp.transpose(mine.reshape(drop_count, 3, point_count), (1, 0, 2))
    return (traction_coeffs, split_traction, near_velocity.reshape(3, drop_count * point_count))


def near_kernel(t_ref, r_ref, q_ref, n_ref, w_ref, o_ref, s_ref):
    drop = pl.program_id(0)
    targets = o_ref.shape[2]
    chunks = r_ref.shape[1] // 8
    r = r_ref[0]
    s_ref[0] = r * n_ref[0]
    s_ref[1] = r * n_ref[1]
    s_ref[2] = r * n_ref[2]
    s_ref[3] = q_ref[0] * r * r * w_ref[...]

    def body(t, carry):
        base = (drop * targets + t) * 3
        tx = t_ref[base]
        ty = t_ref[base + 1]
        tz = t_ref[base + 2]
        ax = jnp.zeros((8, 128), jnp.float32)
        ay = jnp.zeros((8, 128), jnp.float32)
        az = jnp.zeros((8, 128), jnp.float32)
        for c in range(chunks):
            rows = pl.ds(c * 8, 8)
            nx = n_ref[0, rows, :]
            ny = n_ref[1, rows, :]
            nz = n_ref[2, rows, :]
            dx = tx - s_ref[0, rows, :]
            dy = ty - s_ref[1, rows, :]
            dz = tz - s_ref[2, rows, :]
            dd = dx * dx + dy * dy + dz * dz
            inv = lax.rsqrt(dd + SOFTENING)
            w = s_ref[3, rows, :] * (inv * inv * inv)
            dn = dx * nx + dy * ny + dz * nz
            a = dd + 2.0 * SOFTENING
            ax = ax + w * (nx * a + dx * dn)
            ay = ay + w * (ny * a + dy * dn)
            az = az + w * (nz * a + dz * dn)
        o_ref[0, 0, pl.ds(t, 1), :] = jnp.sum(ax, axis=0, keepdims=True)
        o_ref[0, 1, pl.ds(t, 1), :] = jnp.sum(ay, axis=0, keepdims=True)
        o_ref[0, 2, pl.ds(t, 1), :] = jnp.sum(az, axis=0, keepdims=True)
        return carry

    lax.fori_loop(0, targets, body, 0)


def near_field(target_point, source_radius, source_traction, normals, cell_weight):
    drops, nlat, nlon = source_radius.shape
    targets = target_point.shape[0] // (3 * drops)
    cells = drops * targets * nlat * nlon
    return pl.pallas_call(
        near_kernel,
        grid=(drops,),
        in_specs=[
            pl.BlockSpec(memory_space=pltpu.SMEM),
            pl.BlockSpec((1, nlat, nlon), lambda s: (s, 0, 0)),
            pl.BlockSpec((1, nlat, nlon), lambda s: (s, 0, 0)),
            pl.BlockSpec((3, nlat, nlon), lambda s: (0, 0, 0)),
            pl.BlockSpec((nlat, nlon), lambda s: (0, 0)),
        ],
        out_specs=pl.BlockSpec((1, 3, targets, nlon), lambda s: (s, 0, 0, 0)),
        out_shape=jax.ShapeDtypeStruct((drops, 3, targets, nlon), jnp.float32),
        scratch_shapes=[pltpu.VMEM((4, nlat, nlon), jnp.float32)],
        cost_estimate=pl.CostEstimate(
            flops=36 * cells, transcendentals=cells, bytes_accessed=4 * drops * nlat * nlon * 2
        ),
    )(target_point, source_radius, source_traction, normals, cell_weight)


def solution(mesh):
    in_specs = (
        P(("row", "col"), None, None, None),
        P(("row", "col")),
        P(("row", "col"), None),
        P(("row", "col"), None, None, None),
        P(),
        P(None, ("row", "col"), None),
        P(("row", "col"), None),
        P(("row", "col"), None),
    )
    out_specs = (
        P(("row", "col"), None, None),
        P(("row", "col"), None, None),
        P(None, ("row", "col")),
    )
    return jax.shard_map(
        per_device, mesh=mesh, in_specs=in_specs, out_specs=out_specs, check_vma=False
    )
```

profile of v0, /device:TPU:0, one launch (start us, length us, event | category | flops | bytes accessed | tf_op | source)
XLA Modules:
  0.0 798.4 jit_solution(15872332362399012940)
XLA Ops:
  7.2 0.0 copy-start
  7.2 0.0 reduce-scatter.2.cloned.1.call-start
  7.3 0.7 fusion.44
  8.0 1.7 broadcast_multiply_fusion
  9.7 0.2 pad_maximum_fusion
  10.0 3.8 reshape_reshape.6
  13.7 7.7 copy.82
  21.4 7.0 convolution_bitcast_fusion
  28.4 7.4 copy.83
  35.7 5.4 dot_general.33
  41.2 3.4 fusion
  44.6 1.3 copy-done.2
  45.9 1.2 bitcast_convert_fusion.1
  47.1 0.1 pad_maximum_fusion.2
  47.1 0.2 slice.84
  47.3 0.1 copy.102
  47.4 58.0 %all-gather = bf16[128,16,4]{1,2,0:T(4,128)(2,1)S(1)} all-gather(bf16[1,16,4]{1,2,0:T(4,128)(2,1)S(1)} %bitcast.117), channel_id=1, replica_groups=mesh['row'=8,'col'=16] {'row','col'}, dimensions={0}, use_global_device_ids=true | all-gather | bytes 16512 | tf_op jit(solution)/shard_map/all_gather | solution.py:202
  105.4 0.2 reshape.197
  105.6 0.1 copy.99
  105.7 0.1 eq.21
  105.8 0.4 fusion.7
  106.1 0.1 mul.353
  106.2 0.1 copy.100
  106.3 0.1 add.123
  106.4 0.1 add.124
  106.5 0.1 add.125
  106.7 0.1 mul.357
  106.8 0.2 copy.105
  107.0 0.8 reshape.190.t_ref
  107.8 0.7 broadcast_in_dim.2.w_ref
  108.5 29.6 %shard_map.139 = f32[16,3,32,128]{3,2,1,0:T(8,128)} custom-call(f32[1536]{0:T(1024)} %reshape.190.t_ref, f32[16,64,128]{2,1,0:T(8,128)} %get-tuple-element.14.r_ref, f32[16,64,128]{2,1,0:T(8,128)} %get-tuple-element.20.q_ref, f32[3,64,128]{2,1,0:T(8,128)} %constant.106.clone.n_ref, f32[64,128]{1,0:T(8,128)} %broadcast_in_dim.2.w_ref), custom_call_target="tpu_custom_call" | custom-call | flops 150994944 | bytes 1048576 | tf_op jit(solution)/shard_map/pallas_call | solution.py:276
  138.1 1.5 reduce_sum.9
  139.6 0.1 copy.107
  139.6 0.1 copy.108
  139.8 0.1 reshape.191
  139.9 1.7 fusion.15
  141.6 0.0 reduce-scatter.2.cloned.1.call-update
  141.6 0.1 fusion.41
  141.7 0.1 fusion.42
  141.8 0.0 copy-done.5
  141.8 0.1 copy.119
  141.9 0.1 copy.120
  142.0 0.1 copy.118
  142.3 3.2 convolution_bitcast_fusion.3
  145.5 2.0 fusion.55
  147.5 2.8 convolution_multiply_fusion
  150.3 1.6 reshape.184
  151.9 1.4 copy.87
  153.4 3.3 convolution_bitcast_fusion.1
  156.7 0.7 copy.88
  157.4 0.6 reshape.185
  158.0 1.0 multiply_multiply_fusion.5
  159.0 0.1 constant_dynamic-slice_fusion.1
  159.0 627.2 %reduce-scatter.2.cloned.1.call-done = f32[16,12]{1,0:T(8,128)} async-done(((f32[2048,12]{1,0:T(8,128)}), f32[16,12]{1,0:T(8,128)}) %reduce-scatter.2.cloned.1.call-update) | async-done | bytes 784 | tf_op jit(solution)/shard_map/reduce_scatter | solution.py:225
  786.2 0.8 copy.109
  787.0 0.1 copy.110
  787.1 0.7 reshape.193
  787.8 1.0 convert_add_fusion
  788.8 0.3 convolution_multiply_fusion.1
  789.1 0.2 reshape.188
  789.3 0.3 constant_dynamic-slice_fusion
  789.6 0.1 copy.124
  789.8 1.0 convolution_bitcast_fusion.4
  790.8 0.8 copy.111
  (47 shorter events, 0.3 us)
Async XLA Ops:
  7.2 151.8 %copy-start = (f32[256,2]{0,1:T(2,128)S(1)}, f32[256,2]{0,1:T(2,128)}, u32[]{:S(2)}) copy-start(f32[256,2]{0,1:T(2,128)} %param.16) | copy-start | bytes 6148
  7.2 779.0 %reduce-scatter.2.cloned.1.call-start = ((), (), s32[]{:S(2)}) async-start(), calls=%async_computation.1 | async-start | bytes 1056768 | tf_op jit(solution)/shard_map/reduce_scatter | solution.py:225
  13.7 7.7 copy-start.1
  35.7 5.4 copy-start.14
  35.7 5.5 copy-start.6
  44.6 1.3 copy-start.2
  45.9 59.7 %copy-start.10 = (s32[16,8]{0,1:T(8,128)S(1)}, s32[16,8]{0,1:T(8,128)}, u32[]{:S(2)}) copy-start(s32[16,8]{0,1:T(8,128)} %param.19) | copy-start | bytes 1540
  45.9 59.7 %copy-start.11 = (s32[16,8]{0,1:T(8,128)S(1)}, s32[16,8]{0,1:T(8,128)}, u32[]{:S(2)}) copy-start(s32[16,8]{0,1:T(8,128)} %param.18) | copy-start | bytes 1540
  45.9 60.3 %copy-start.9 = (f32[3,16,8]{1,2,0:T(8,128)S(1)}, f32[3,16,8]{1,2,0:T(8,128)}, u32[]{:S(2)}) copy-start(f32[3,16,8]{1,2,0:T(8,128)} %param.17) | copy-start | bytes 4612
  47.1 59.6 %copy-start.12 = (f32[3,4]{1,0:T(4,128)S(1)}, f32[3,4]{1,0:T(4,128)}, u32[]{:S(2)}) copy-start(f32[3,4]{1,0:T(4,128)} %constant.116) | copy-start | bytes 148
  47.1 60.7 %copy-start.13 = (f32[64]{0:T(128)S(1)}, f32[64]{0:T(128)}, u32[]{:S(2)}) copy-start(f32[64]{0:T(128)} %constant.105.clone) | copy-start | bytes 772
  138.1 3.7 copy-start.5
  142.1 3.3 copy-start.8
  142.2 5.2 copy-start.7
  147.5 640.3 %collective-permute-start = (bf16[16,64,128]{2,1,0:T(8,128)(2,1)S(1)}, bf16[16,64,128]{2,1,0:T(8,128)(2,1)}, u32[]{:S(2)}, u32[]{:S(2)}) collective-permute-start(bf16[16,64,128]{2,1,0:T(8,128)(2,1)S(1)} %get-tuple-element.33), channel_id=1, source_target_pairs={{0,16},{16,0},{32,48},{48,32},{64,80},{80,64},{96,112},{112,96},{1... | collective-permute-start | bytes 786440 | tf_op jit(solution)/shard_map/ppermute | solution.py:22
  157.3 630.4 %copy-start.4 = (f32[16,64,128]{2,1,0:T(8,128)S(1)}, f32[16,64,128]{2,1,0:T(8,128)}, u32[]{:S(2)}) copy-start(f32[16,64,128]{2,1,0:T(8,128)} %get-tuple-element.34) | copy-start | bytes 1572868
  157.9 631.9 %copy-start.3 = (f32[64,64,64]{2,1,0:T(8,128)S(1)}, f32[64,64,64]{2,1,0:T(8,128)}, u32[]{:S(2)}) copy-start(f32[64,64,64]{2,1,0:T(8,128)} %constant.103.clone) | copy-start | bytes 3145732
Sparse Core Ops, SparseCore 0:
  141.7 644.4 reduce-scatter.1
where the time goes:
time: 799 us; the launch traced here: 798 us
  waiting for transfers between devices  627 us (78%)
  blocking collectives  58 us (7%)
  local copies, waits for them, and re-layouts  36.5 us (5%)
  Pallas kernels  29.6 us (4%)
  matrix products  25 us (3%)
  between operations  14.4 us (2%)
    reduce_scatter x1, waiting for transfers between devices, per_device(): lax.psum_scatter(dense, ('row', 'col'), scatter_dimension=0, tiled=True)  627 us
    all_gather x1, blocking collectives, per_device(): all_points = lax.all_gather(own_points, ('row', 'col'), axis=0, tiled=True)  58 us
    pallas_call x1, Pallas kernels, near_field(): pl.pallas_call(near_kernel, grid=(drops,), in_specs=[pl.BlockSpec(memory_...  29.6 us
  transfers between devices with their start and end apart: 2, of which 1 were waited for; matrix products, arithmetic and copies ran while one was open for 2% of the time, Pallas kernels for 0%

commit v1 on v0

--- a/solution.py
+++ b/solution.py
@@ -199,7 +199,14 @@
     point_count = point_grid.shape[1] * point_grid.shape[2]
     own_points = point_grid.reshape(drop_count, point_count)
     target_normal = normals[:, nlat // 4 :: nlat // 2, :: nlon // 2].reshape(3, point_count)
-    all_points = lax.all_gather(own_points, ("row", "col"), axis=0, tiled=True)
+    devices = lax.axis_size("row") * lax.axis_size("col")
+    all_points = lax.all_to_all(
+        jnp.broadcast_to(own_points.reshape(1, -1), (devices, drop_count * point_count)),
+        ("row", "col"),
+        split_axis=0,
+        concat_axis=0,
+        tiled=True,
+    ).reshape(devices * drop_count, point_count)
     total_drops = all_points.shape[0]
     readers = reader_dev.shape[1]
     target = (reader_dev * drop_count + reader_slot).reshape(-1)
@@ -221,8 +228,31 @@
     contribution = jnp.transpose(
         contribution.reshape(drop_count, 3, readers, point_count), (0, 2, 1, 3)
     ).reshape(drop_count * readers, 3 * point_count)
-    dense = jnp.dot(jnp.transpose(pick), contribution, precision=HIGH)
-    mine = lax.psum_scatter(dense, ("row", "col"), scatter_dimension=0, tiled=True)
+    destination = reader_dev.reshape(-1)
+    capacity = 2
+    onehot = (destination[:, None] == jnp.arange(devices, dtype=jnp.int32)[None, :]).astype(
+        jnp.int32
+    )
+    rank = jnp.sum((jnp.cumsum(onehot, axis=0) - onehot) * onehot, axis=1)
+    position = destination * capacity + rank
+    place = (position[:, None] == jnp.arange(devices * capacity, dtype=jnp.int32)[None, :]).astype(
+        jnp.float32
+    )
+    record = jnp.concatenate(
+        [contribution, reader_slot.reshape(-1, 1).astype(jnp.float32)], axis=1
+    )
+    outgoing = jnp.dot(jnp.transpose(place), record, precision=HIGH)
+    incoming = lax.all_to_all(
+        outgoing.reshape(devices, capacity, record.shape[1]),
+        ("row", "col"),
+        split_axis=0,
+        concat_axis=0,
+        tiled=True,
+    ).reshape(devices * capacity, record.shape[1])
+    slot_pick = (
+        incoming[:, -1:] == jnp.arange(drop_count, dtype=jnp.float32)[None, :]
+    ).astype(jnp.float32)
+    mine = jnp.dot(jnp.transpose(slot_pick), incoming[:, :-1], precision=HIGH)
     near_velocity = jnp.transpose(mine.reshape(drop_count, 3, point_count), (1, 0, 2))
     return (traction_coeffs, split_traction, near_velocity.reshape(3, drop_count * point_count))
 

time: 799 us -> 134 us (0.17)
  waiting for transfers between devices: 627 us -> 9.57 us
  blocking collectives: 58 us -> 0 us
  starting transfers between devices: 0.04 us -> 21.1 us
  between operations: 14.4 us -> 1.15 us
    reduce_scatter x1 -> x0, waiting for transfers between devices: 627 us -> none  [per_device(): lax.psum_scatter(dense, ('row', 'col'), scatter_dimension=0, tiled=True)]
    all_gather x1 -> x0, blocking collectives: 58 us -> none  [per_device(): all_points = lax.all_gather(own_points, ('row', 'col'), axis=0, tiled=True)]
    all_to_all x0 -> x2, starting transfers between devices: none -> 21.1 us  [the longest x1 11.3 us: per_device(): lax.all_to_all(jnp.broadcast_to(own_points.reshape(1, -1), (devices, drop...]
    all_to_all x0 -> x2, waiting for transfers between devices: none -> 9.56 us  [the longest x1 9.56 us: per_device(): lax.all_to_all(outgoing.reshape(devices, capacity, record.shape[1]), ('ro...]
  transfers between devices with their start and end apart: 2 -> 3, of which waited for: 1 -> 1; matrix products, arithmetic and copies ran while one was open for 2% -> 20% of each run, Pallas kernels for 0% -> 22%
where the time goes in v1:
time: 134 us; the launch traced here: 133 us
  local copies, waits for them, and re-layouts  37.4 us (28%)
  Pallas kernels  29.6 us (22%)
  matrix products  24.6 us (18%)
  starting transfers between devices  21.1 us (16%)
  waiting for transfers between devices  9.57 us (7%)
  other arithmetic  9.4 us (7%)
    pallas_call x1, Pallas kernels, near_field(): pl.pallas_call(near_kernel, grid=(drops,), in_specs=[pl.BlockSpec(memory_...  29.6 us
    another operation x2, local copies, waits for them, and re-layouts, legendre_synth(): parted = coeff.reshape(batch_size, degrees, 2, orders)  11.4 us
    all_to_all x1, starting transfers between devices, per_device(): lax.all_to_all(jnp.broadcast_to(own_points.reshape(1, -1), (devices, drop...  11.3 us
    dot_general x2, matrix products, legendre_synth(): return jnp.einsum('mjl,nlcm->njcm', legendre, parted, precision=HIGH)  10.2 us
    all_to_all x1, starting transfers between devices, per_device(): lax.all_to_all(outgoing.reshape(devices, capacity, record.shape[1]), ('ro...  9.71 us
    all_to_all x1, waiting for transfers between devices, per_device(): lax.all_to_all(outgoing.reshape(devices, capacity, record.shape[1]), ('ro...  9.56 us
    transpose x1, local copies, waits for them, and re-layouts, legendre_synth(): return jnp.einsum('mjl,nlcm->njcm', legendre, parted, precision=HIGH)  7.38 us
    dot_general x1, local copies, waits for them, and re-layouts, fourier_synth(): jnp.einsum('njw,wk->njk', partial_legendre.reshape(batch_size, nlat, two...  5.45 us
  transfers between devices with their start and end apart: 3, of which 1 were waited for; matrix products, arithmetic and copies ran while one was open for 20% of the time, Pallas kernels for 22%

profile of v1, /device:TPU:0, one launch (start us, length us, event | category | flops | bytes accessed | tf_op | source)
XLA Modules:
  0.0 132.8 jit_solution(1125093397439919100)
XLA Ops:
  0.7 0.7 fusion.51
  1.4 1.7 %broadcast_multiply_fusion = (f32[16,1,64,128]{3,2,1,0:T(8,128)S(1)}, f32[16,1,64,128]{3,2,1,0:T(8,128)S(1)}, f32[16,1,64,128]{3,2,1,0:T(8,128)S(1)}, f32[16,1,64,128]{3,2,1,0:T(8,128)S(1)}) fusion(f32[64]{0:T(128)S(1)} %get-tuple-element.40, f32[16,64]{1,0:T(8,128)S(1)} %fusion.51, f32[64,128]{1,0:T(8,128)S(1)} %fusion.47, f32[16,3,64,128]{3,2,1,0:T(8,128)} %param.12, ...), kind=kLoop, calls=%fused_computation.46 | loop fusion | flops 1048576 | bytes 3707392 | tf_op jit(solution)/shard_map/mul | solution.py:111
  3.1 0.2 pad_maximum_fusion
  3.4 3.8 %reshape_reshape.6 = f32[64,64,2,64]{3,2,1,0:T(2,128)} reshape(f32[16,4,64,128]{3,2,1,0:T(8,128)S(1)} %pad_maximum_fusion) | data formatting | bytes 4194304 | tf_op jit(solution)/shard_map/reshape;reshape | solution.py:77
  7.1 7.6 %copy.115 = f32[64,64,2,64]{1,0,2,3:T(8,128)} copy(f32[64,64,2,64]{3,2,1,0:T(2,128)} %reshape_reshape.6) | data formatting | bytes 4194304 | tf_op jit(solution)/shard_map/reshape;reshape | solution.py:77
  14.8 7.0 %convolution_bitcast_fusion = f32[64,64,2,64]{1,0,2,3:T(8,128)} fusion(f32[64,64,2,64]{1,0,2,3:T(8,128)} %copy.115, f32[64,64,64,1]{2,1,3,0:T(8,128)S(1)} %copy-done.1), kind=kOutput, calls=%fused_computation | convolution fusion | flops 402653184 | bytes 5242880 | tf_op jit(solution)/shard_map/mjl,nlcm->njcm/dot_general | solution.py:78
  21.7 7.4 %copy.116 = f32[64,64,2,64]{3,2,1,0:T(2,128)} copy(f32[64,64,2,64]{1,0,2,3:T(8,128)} %convolution_bitcast_fusion) | data formatting | bytes 4194304 | tf_op jit(solution)/shard_map/mjl,nlcm->njcm/transpose | solution.py:78
  29.1 5.5 %dot_general.36 = f32[16,4,64,128]{3,2,1,0:T(8,128)} reshape(f32[64,64,2,64]{3,2,1,0:T(2,128)} %copy.116) | data formatting | bytes 4194304 | tf_op jit(solution)/shard_map/njw,wk->njk/dot_general | solution.py:83
  34.6 3.4 %fusion = f32[16,4,64,128]{3,2,0,1:T(8,128)S(1)} fusion(f32[128,128,1,1]{1,0,2,3:T(8,128)S(1)} %copy-done.6, f32[16,4,64,128]{3,2,1,0:T(8,128)} %dot_general.36), kind=kOutput, calls=%fused_computation.2 | convolution fusion | flops 805306368 | bytes 4259840 | tf_op jit(solution)/shard_map/njw,wk->njk/dot_general | solution.py:83
  38.0 1.3 %copy-done.2 = f32[16,4,64,128]{3,2,0,1:T(8,128)} copy-done((f32[16,4,64,128]{3,2,0,1:T(8,128)}, f32[16,4,64,128]{3,2,0,1:T(8,128)S(1)}, u32[]{:S(2)}) %copy-start.2) | copy-done | bytes 2097176
  39.3 1.2 bitcast_convert_fusion.1
  40.5 0.2 slice.90
  40.7 0.1 broadcast_in_dim.6
  40.8 0.7 broadcast_in_dim.7
  41.5 11.3 %all-to-all-start = ((bf16[128,1,64]{2,1,0:T(2,128)(2,1)}), bf16[128,1,64]{2,1,0:T(2,128)(2,1)S(1)}, u32[]{:S(2)}, u32[]{:S(2)}) async-start(bf16[128,1,64]{2,1,0:T(2,128)(2,1)} %broadcast_in_dim.7), calls=%async_computation | async-start | bytes 131072 | tf_op jit(solution)/shard_map/all_to_all | solution.py:203
  53.1 0.1 copy.155
  53.2 0.1 copy.156
  53.3 0.1 copy.154
  53.6 3.2 %convolution_bitcast_fusion.3 = f32[16,64,2,32]{1,0,2,3:T(8,128)S(1)} fusion(f32[64,64,64]{2,1,0:T(8,128)} %constant.108.clone, s32[]{:T(128)S(6)} %select_n.46, f32[16,64,2,32]{1,3,2,0:T(8,128)S(1)} %bitcast.113), kind=kOutput, calls=%fused_computation.6 | convolution fusion | flops 50331648 | bytes 1572868 | tf_op jit(solution)/shard_map/mjl,nlcm->njcm/dot_general | solution.py:78
  56.8 2.0 %fusion.63 = (bf16[16,64,128]{2,1,0:T(8,128)(2,1)S(1)}, f32[16,64,128]{2,1,0:T(8,128)}) fusion(f32[2,64,128]{2,1,0:T(8,128)S(1)} %copy-done.9, s32[]{:T(128)S(6)} %select_n.46, f32[16,64,2,32]{1,0,2,3:T(8,128)S(1)} %convolution_bitcast_fusion.3), kind=kOutput, calls=%fused_computation.111 | convolution fusion | flops 100794368 | bytes 1343492 | tf_op jit(solution)/shard_map/njw,wk->njk/dot_general | solution.py:83
  58.9 0.6 multiply_add_fusion
  59.4 0.1 reshape.234
  59.5 0.1 fusion.39
  59.6 0.2 reduce_window_sum.11
  59.8 0.2 select_reduce_fusion
  60.0 0.5 multiply_add_fusion.1
  60.5 2.8 %convolution_multiply_fusion = f32[16,64,128]{2,1,0:T(8,128)} fusion(f32[128,128,1]{1,0,2:T(8,128)S(1)} %copy-done.7, f32[16,4,64,128]{3,2,0,1:T(8,128)} %copy-done.2, f32[64]{0:T(128)S(1)} %copy-done.15, f32[16]{0:T(128)S(1)} %get-tuple-element.37, f32[16]{0:T(128)S(1)} %get-tuple-element.36), kind=kOutput, calls=%fused_computation.7 | convolution fusion | flops 202244096 | bytes 2163072 | tf_op jit(solution)/shard_map/bjk,wk->bjw/dot_general | solution.py:94
  63.3 1.6 %reshape.228 = f32[16,64,2,64]{3,2,1,0:T(2,128)S(1)} reshape(f32[16,64,128]{2,1,0:T(8,128)} %convolution_multiply_fusion) | data formatting | bytes 1048576 | tf_op jit(solution)/shard_map/reshape | solution.py:97
  65.0 1.4 %copy.120 = f32[16,64,2,64]{1,0,2,3:T(8,128)} copy(f32[16,64,2,64]{3,2,1,0:T(2,128)S(1)} %reshape.228) | data formatting | bytes 1048576 | tf_op jit(solution)/shard_map/reshape | solution.py:97
  66.4 3.3 %convolution_bitcast_fusion.1 = f32[16,64,2,64]{1,0,2,3:T(8,128)S(1)} fusion(f32[16,64,2,64]{1,0,2,3:T(8,128)} %copy.120, f32[64,64,64,1]{2,1,3,0:T(8,128)S(1)} %copy-done.1), kind=kOutput, calls=%fused_computation.4 | convolution fusion | flops 100663296 | bytes 2097152 | tf_op jit(solution)/shard_map/mjl,bjcm->blcm/dot_general | solution.py:102
  69.7 0.7 copy.121
  70.4 0.6 reshape.229
  71.0 1.0 multiply_multiply_fusion.5
  72.2 0.1 eq.68
  72.3 0.1 add.128
  72.4 0.1 add.129
  72.5 0.1 add.130
  72.7 0.1 mul.373
  72.9 0.1 convert_element_type.73
  73.0 0.2 reduce
  73.2 0.6 reshape.235
  73.8 0.4 fusion.6
  74.2 0.1 mul.369
  74.2 0.2 copy.137
  74.4 0.8 reshape.236.t_ref
  75.3 0.7 broadcast_in_dim.8.w_ref
  75.9 29.6 %shard_map.139 = f32[16,3,32,128]{3,2,1,0:T(8,128)} custom-call(f32[1536]{0:T(1024)} %reshape.236.t_ref, f32[16,64,128]{2,1,0:T(8,128)} %get-tuple-element.17.r_ref, f32[16,64,128]{2,1,0:T(8,128)} %get-tuple-element.23.q_ref, f32[3,64,128]{2,1,0:T(8,128)} %constant.111.clone.n_ref, f32[64,128]{1,0:T(8,128)} %broadcast_in_dim.8.w_ref), custom_call_target="tpu_custom_call" | custom-call | flops 150994944 | bytes 1048576 | tf_op jit(solution)/shard_map/pallas_call | solution.py:306
  105.6 1.5 %reduce_sum.19 = f32[16,3,32]{2,1,0:T(4,128)S(1)} reduce(f32[16,3,32,128]{3,2,1,0:T(8,128)} %shard_map.139, f32[]{:T(128)} %constant.106.clone.1), dimensions={3}, to_apply=%region_2.3 | reduce | flops 195072 | bytes 792580 | tf_op jit(solution)/shard_map/reduce_sum | solution.py:227
  107.2 0.1 copy.140
  107.3 0.1 reshape.237
  107.4 1.0 fusion.35
  108.4 9.7 %all-to-all-start.1 = ((f32[128,2,13]{2,1,0:T(2,128)}), f32[128,2,13]{2,1,0:T(2,128)S(1)}, u32[]{:S(2)}, u32[]{:S(2)}) async-start(f32[128,2,13]{2,1,0:T(2,128)} %bitcast.31), calls=%async_computation.1 | async-start | bytes 262144 | tf_op jit(solution)/shard_map/all_to_all | solution.py:245
  118.1 9.6 %all-to-all-done.1 = f32[128,2,13]{2,1,0:T(2,128)S(1)} async-done(((f32[128,2,13]{2,1,0:T(2,128)}), f32[128,2,13]{2,1,0:T(2,128)S(1)}, u32[]{:S(2)}, u32[]{:S(2)}) %all-to-all-start.1) | async-done | bytes 13344 | tf_op jit(solution)/shard_map/all_to_all | solution.py:245
  127.7 0.2 slice_reduce_fusion
  127.8 0.3 fusion.28
  128.2 0.1 copy.144
  128.3 0.7 reshape.241
  128.9 1.0 convert_add_fusion
  130.0 0.3 convolution_multiply_fusion.1
  130.3 0.2 reshape.232
  130.5 0.3 constant_dynamic-slice_fusion
  130.8 0.1 copy.160
  131.0 1.0 convolution_bitcast_fusion.4
  132.0 0.8 copy.145
  (65 shorter events, 1.0 us)
Async XLA Ops:
  0.6 71.4 %copy-start = (f32[256,2]{0,1:T(2,128)S(1)}, f32[256,2]{0,1:T(2,128)}, u32[]{:S(2)}) copy-start(f32[256,2]{0,1:T(2,128)} %param.16) | copy-start | bytes 6148
  7.1 7.6 %copy-start.1 = (f32[64,64,64,1]{2,1,3,0:T(8,128)S(1)}, f32[64,64,64,1]{2,1,3,0:T(8,128)}, u32[]{:S(2)}) copy-start(f32[64,64,64,1]{2,1,3,0:T(8,128)} %constant.122) | copy-start | bytes 3145732
  29.1 5.5 %copy-start.17 = (f32[16,2]{0,1:T(2,128)S(1)}, f32[16,2]{0,1:T(2,128)}, u32[]{:S(2)}) copy-start(f32[16,2]{0,1:T(2,128)} %param.14) | copy-start | bytes 388
  29.1 5.5 %copy-start.6 = (f32[128,128,1,1]{1,0,2,3:T(8,128)S(1)}, f32[128,128,1,1]{1,0,2,3:T(8,128)}, u32[]{:S(2)}) copy-start(f32[128,128,1,1]{1,0,2,3:T(8,128)} %constant.123) | copy-start | bytes 196612
  38.0 1.3 %copy-start.2 = (f32[16,4,64,128]{3,2,0,1:T(8,128)}, f32[16,4,64,128]{3,2,0,1:T(8,128)S(1)}, u32[]{:S(2)}) copy-start(f32[16,4,64,128]{3,2,0,1:T(8,128)S(1)} %fusion) | copy-start | bytes 6291460
  39.3 13.7 %copy-start.5 = (f32[4,3,64,64]{3,2,1,0:T(8,128)S(1)}, f32[4,3,64,64]{3,2,1,0:T(8,128)}, u32[]{:S(2)}) copy-start(f32[4,3,64,64]{3,2,1,0:T(8,128)} %param.15) | copy-start | bytes 589828
  41.5 31.5 %all-to-all-start = ((bf16[128,1,64]{2,1,0:T(2,128)(2,1)}), bf16[128,1,64]{2,1,0:T(2,128)(2,1)S(1)}, u32[]{:S(2)}, u32[]{:S(2)}) async-start(bf16[128,1,64]{2,1,0:T(2,128)(2,1)} %broadcast_in_dim.7), calls=%async_computation | async-start | bytes 131072 | tf_op jit(solution)/shard_map/all_to_all | solution.py:203
  53.4 3.4 %copy-start.9 = (f32[2,64,128]{2,1,0:T(8,128)S(1)}, f32[2,64,128]{2,1,0:T(8,128)}, u32[]{:S(2)}) copy-start(f32[2,64,128]{2,1,0:T(8,128)} %constant.119) | copy-start | bytes 196612
  53.5 5.3 %copy-start.10 = (s32[16,8]{0,1:T(8,128)S(1)}, s32[16,8]{0,1:T(8,128)}, u32[]{:S(2)}) copy-start(s32[16,8]{0,1:T(8,128)} %param.18) | copy-start | bytes 1540
  53.5 5.4 %copy-start.13 = (s32[16,8]{0,1:T(8,128)S(1)}, s32[16,8]{0,1:T(8,128)}, u32[]{:S(2)}) copy-start(s32[16,8]{0,1:T(8,128)} %param.19) | copy-start | bytes 1540
  53.5 7.0 %copy-start.7 = (f32[128,128,1]{1,0,2:T(8,128)S(1)}, f32[128,128,1]{1,0,2:T(8,128)}, u32[]{:S(2)}) copy-start(f32[128,128,1]{1,0,2:T(8,128)} %constant.124) | copy-start | bytes 196612
  53.5 7.0 %copy-start.15 = (f32[64]{0:T(128)S(1)}, f32[64]{0:T(128)}, u32[]{:S(2)}) copy-start(f32[64]{0:T(128)} %constant.110.clone) | copy-start | bytes 772
  58.8 70.2 %collective-permute-start = (bf16[16,64,128]{2,1,0:T(8,128)(2,1)S(1)}, bf16[16,64,128]{2,1,0:T(8,128)(2,1)}, u32[]{:S(2)}, u32[]{:S(2)}) collective-permute-start(bf16[16,64,128]{2,1,0:T(8,128)(2,1)S(1)} %get-tuple-element.38), channel_id=1, source_target_pairs={{0,16},{16,0},{32,48},{48,32},{64,80},{80,64},{96,112},{112,96},{1... | collective-permute-start | bytes 786440 | tf_op jit(solution)/shard_map/ppermute | solution.py:22
  69.7 2.4 %copy-start.11 = (s32[16,8]{0,1:T(8,128)S(1)}, s32[16,8]{0,1:T(8,128)}, u32[]{:S(2)}) copy-start(s32[16,8]{0,1:T(8,128)} %get-tuple-element.32) | copy-start | bytes 1540
  69.7 2.5 %copy-start.12 = (f32[3,16,8]{1,2,0:T(8,128)S(1)}, f32[3,16,8]{1,2,0:T(8,128)}, u32[]{:S(2)}) copy-start(f32[3,16,8]{1,2,0:T(8,128)} %param.17) | copy-start | bytes 4612
  70.4 2.3 %copy-start.14 = (f32[3,4]{1,0:T(4,128)S(1)}, f32[3,4]{1,0:T(4,128)}, u32[]{:S(2)}) copy-start(f32[3,4]{1,0:T(4,128)} %constant.121) | copy-start | bytes 148
  71.0 4.3 %copy-start.16 = (f32[64]{0:T(128)S(1)}, f32[64]{0:T(128)}, u32[]{:S(2)}) copy-start(f32[64]{0:T(128)} %constant.110.clone) | copy-start | bytes 772
  75.9 31.4 %copy-start.18 = (s32[128]{0:T(128)S(1)}, s32[128]{0:T(128)}, u32[]{:S(2)}) copy-start(s32[128]{0:T(128)} %multiply_add_fusion.1) | copy-start | bytes 1540
  105.6 23.4 %copy-start.4 = (f32[16,64,128]{2,1,0:T(8,128)S(1)}, f32[16,64,128]{2,1,0:T(8,128)}, u32[]{:S(2)}) copy-start(f32[16,64,128]{2,1,0:T(8,128)} %get-tuple-element.39) | copy-start | bytes 1572868
  105.6 24.4 %copy-start.8 = (f32[128,128,1]{1,0,2:T(8,128)S(1)}, f32[128,128,1]{1,0,2:T(8,128)}, u32[]{:S(2)}) copy-start(f32[128,128,1]{1,0,2:T(8,128)} %constant.124) | copy-start | bytes 196612
  107.1 23.9 %copy-start.3 = (f32[64,64,64]{2,1,0:T(8,128)S(1)}, f32[64,64,64]{2,1,0:T(8,128)}, u32[]{:S(2)}) copy-start(f32[64,64,64]{2,1,0:T(8,128)} %constant.108.clone) | copy-start | bytes 3145732
  108.4 19.3 %all-to-all-start.1 = ((f32[128,2,13]{2,1,0:T(2,128)}), f32[128,2,13]{2,1,0:T(2,128)S(1)}, u32[]{:S(2)}, u32[]{:S(2)}) async-start(f32[128,2,13]{2,1,0:T(2,128)} %bitcast.31), calls=%async_computation.1 | async-start | bytes 262144 | tf_op jit(solution)/shard_map/all_to_all | solution.py:245

commit v2 on v1

--- a/solution.py
+++ b/solution.py
@@ -9,6 +9,7 @@
 from jax.sharding import PartitionSpec as P
 
 HIGH = lax.Precision.HIGHEST
+SPECTRAL = lax.Precision.DEFAULT
 SOFTENING = 0.04
 
 
@@ -75,7 +76,7 @@
     batch_size, degrees, coef_width = coeff.shape
     orders = legendre.shape[0]
     parted = coeff.reshape(batch_size, degrees, 2, orders)
-    return jnp.einsum("mjl,nlcm->njcm", legendre, parted, precision=HIGH)
+    return jnp.einsum("mjl,nlcm->njcm", legendre, parted, precision=SPECTRAL)
 
 
 def fourier_synth(partial_legendre, fourier_rows):
@@ -84,14 +85,14 @@
         "njw,wk->njk",
         partial_legendre.reshape(batch_size, nlat, two * orders),
         fourier_rows,
-        precision=HIGH,
+        precision=SPECTRAL,
     )
 
 
 def analysis_fourier(traction_grid, fourier, quad_weight):
     batch_size, nlat, nlon = traction_grid.shape
     projected = (
-        jnp.einsum("bjk,wk->bjw", traction_grid, fourier, precision=HIGH)
+        jnp.einsum("bjk,wk->bjw", traction_grid, fourier, precision=SPECTRAL)
         * quad_weight[None, :, None]
     )
     return projected.reshape(batch_size, nlat, 2, fourier.shape[0] // 2)
@@ -99,7 +100,7 @@
 
 def analysis_legendre(coef_grid, legendre):
     batch_size = coef_grid.shape[0]
-    result = jnp.einsum("mjl,bjcm->blcm", legendre, coef_grid, precision=HIGH)
+    result = jnp.einsum("mjl,bjcm->blcm", legendre, coef_grid, precision=SPECTRAL)
     return result.reshape(batch_size, legendre.shape[2], 2 * legendre.shape[0])
 
 

time: 134 us -> 114 us (0.85)
  matrix products: 24.6 us -> 9.38 us
  local copies, waits for them, and re-layouts: 37.4 us -> 27.5 us
  other arithmetic: 9.4 us -> 13.9 us
    dot_general x6, matrix products: 17.6 us -> 5.34 us  [the longest x2 2.69 us: legendre_synth(): return jnp.einsum('mjl,nlcm->njcm', legendre, parted, precision=SPECTRAL)]
    another operation x2, local copies, waits for them, and re-layouts: 11.4 us -> 5.22 us  [legendre_synth(): parted = coeff.reshape(batch_size, degrees, 2, orders)]
    dot_general x2, matrix products: 5.38 us -> 2.39 us  [fourier_synth(): jnp.einsum('njw,wk->njk', partial_legendre.reshape(batch_size, nlat, two...]
    transpose x3, local copies, waits for them, and re-layouts: 8.07 us -> 5.22 us  [the longest x1 4.53 us: legendre_synth(): return jnp.einsum('mjl,nlcm->njcm', legendre, parted, precision=SPECTRAL)]
    slice x1, local copies, waits for them, and re-layouts: 0.03 us -> 1.71 us  [prepare(): shape_part = coeffs[:, 0] * keep_mask]
    dot_general x1, local copies, waits for them, and re-layouts: 5.45 us -> 3.9 us  [fourier_synth(): jnp.einsum('njw,wk->njk', partial_legendre.reshape(batch_size, nlat, two...]
    mul x2, other arithmetic: 1.73 us -> 3.18 us  [prepare(): shape_part * (degree_value * (degree_value + 1.0) / (degrees * degrees))[...]
    mul x2, other arithmetic: 0.1 us -> 1.47 us  [prepare(): electric = 3.0 * coeffs[:, 1] * keep_mask]
  transfers between devices with their start and end apart: 3 -> 3, of which waited for: 1 -> 1; matrix products, arithmetic and copies ran while one was open for 20% -> 23% of each run, Pallas kernels for 22% -> 26%
where the time goes in v2:
time: 114 us; the launch traced here: 113 us
  Pallas kernels  29.6 us (26%)
  local copies, waits for them, and re-layouts  27.5 us (24%)
  starting transfers between devices  21.5 us (19%)
  other arithmetic  13.9 us (12%)
  waiting for transfers between devices  9.57 us (8%)
  matrix products  9.38 us (8%)
  between operations  1.25 us (1%)
    pallas_call x1, Pallas kernels, near_field(): pl.pallas_call(near_kernel, grid=(drops,), in_specs=[pl.BlockSpec(memory_...  29.6 us
    all_to_all x1, starting transfers between devices, per_device(): lax.all_to_all(jnp.broadcast_to(own_points.reshape(1, -1), (devices, drop...  11.7 us
    all_to_all x1, starting transfers between devices, per_device(): lax.all_to_all(outgoing.reshape(devices, capacity, record.shape[1]), ('ro...  9.81 us
    all_to_all x1, waiting for transfers between devices, per_device(): lax.all_to_all(outgoing.reshape(devices, capacity, record.shape[1]), ('ro...  9.56 us
    another operation x2, local copies, waits for them, and re-layouts, legendre_synth(): parted = coeff.reshape(batch_size, degrees, 2, orders)  5.22 us
    transpose x1, local copies, waits for them, and re-layouts, legendre_synth(): return jnp.einsum('mjl,nlcm->njcm', legendre, parted, precision=SPECTRAL)  4.53 us
    dot_general x1, local copies, waits for them, and re-layouts, fourier_synth(): jnp.einsum('njw,wk->njk', partial_legendre.reshape(batch_size, nlat, two...  3.9 us
    mul x2, other arithmetic, prepare(): shape_part * (degree_value * (degree_value + 1.0) / (degrees * degrees))[...  3.18 us
  transfers between devices with their start and end apart: 3, of which 1 were waited for; matrix products, arithmetic and copies ran while one was open for 23% of the time, Pallas kernels for 26%

profile of v2, /device:TPU:0, one launch (start us, length us, event | category | flops | bytes accessed | tf_op | source)
XLA Modules:
  0.0 112.8 jit_solution(16858251254832221944)
XLA Ops:
  0.7 0.7 fusion.51
  1.5 1.7 %broadcast_multiply_fusion = (bf16[16,1,64,128]{3,2,1,0:T(8,128)(2,1)S(1)}, bf16[16,1,64,128]{3,2,1,0:T(8,128)(2,1)S(1)}, bf16[16,1,64,128]{3,2,1,0:T(8,128)(2,1)S(1)}, bf16[16,1,64,128]{3,2,1,0:T(8,128)(2,1)S(1)}) fusion(f32[64]{0:T(128)S(1)} %get-tuple-element.40, f32[16,64]{1,0:T(8,128)S(1)} %fusion.51, f32[64,128]{1,0:T(8,128)S(1)} %fusion.47, ...), kind=kLoop, calls=%fused_computation.46 | loop fusion | flops 1572864 | bytes 2658816 | tf_op jit(solution)/shard_map/mul | solution.py:112
  3.2 0.1 pad_maximum_fusion
  3.4 0.8 reshape_reshape.6
  4.2 4.4 %copy.115 = bf16[64,64,2,64]{1,0,2,3:T(8,128)(2,1)} copy(bf16[64,64,2,64]{3,2,1,0:T(2,128)(2,1)S(1)} %reshape_reshape.6) | data formatting | bytes 2097152 | tf_op jit(solution)/shard_map/reshape;reshape | solution.py:78
  8.6 2.3 %convolution_bitcast_fusion = bf16[64,64,2,64]{1,0,2,3:T(8,128)(2,1)S(1)} fusion(bf16[64,64,2,64]{1,0,2,3:T(8,128)(2,1)} %copy.115, bf16[64,64,64,1]{2,1,3,0:T(8,128)(2,1)S(1)} %copy-done.1), kind=kOutput, calls=%fused_computation | convolution fusion | flops 67108864 | bytes 2621440 | tf_op jit(solution)/shard_map/mjl,nlcm->njcm/dot_general | solution.py:79
  10.9 4.5 %copy.116 = bf16[64,64,2,64]{3,2,1,0:T(2,128)(2,1)} copy(bf16[64,64,2,64]{1,0,2,3:T(8,128)(2,1)S(1)} %convolution_bitcast_fusion) | data formatting | bytes 2097152 | tf_op jit(solution)/shard_map/mjl,nlcm->njcm/transpose | solution.py:79
  15.5 3.9 %dot_general.36 = bf16[16,4,64,128]{3,2,1,0:T(8,128)(2,1)S(1)} reshape(bf16[64,64,2,64]{3,2,1,0:T(2,128)(2,1)} %copy.116) | data formatting | bytes 2097152 | tf_op jit(solution)/shard_map/njw,wk->njk/dot_general | solution.py:84
  19.4 0.4 fusion
  19.8 1.2 %bitcast_convert_fusion.1 = (f32[16,64,128]{2,1,0:T(8,128)}, bf16[16,1,64,128]{3,2,0,1:T(8,128)(2,1)S(1)}, f32[16,64,128]{2,1,0:T(8,128)}, bf16[16,1,64,128]{3,2,0,1:T(8,128)(2,1)S(1)}) fusion(f32[16,4,64,128]{3,2,0,1:T(8,128)S(1)} %fusion, f32[16]{0:T(128)S(1)} %get-tuple-element.37, f32[16]{0:T(128)S(1)} %get-tuple-element.36), kind=kLoop, calls=%fused_computation.43 | loop fusion | flops 1310720 | bytes 3670144 | tf_op jit(solution)/shard_map/convert_element_type | solution.py:224
  21.1 0.8 pad_maximum_fusion.2
  21.9 1.1 slice.90
  23.0 0.1 broadcast_in_dim.6
  23.1 0.7 broadcast_in_dim.7
  23.8 11.7 %all-to-all-start = ((bf16[128,1,64]{2,1,0:T(2,128)(2,1)}), bf16[128,1,64]{2,1,0:T(2,128)(2,1)}, u32[]{:S(2)}, u32[]{:S(2)}) async-start(bf16[128,1,64]{2,1,0:T(2,128)(2,1)} %broadcast_in_dim.7), calls=%async_computation | async-start | bytes 131072 | tf_op jit(solution)/shard_map/all_to_all | solution.py:204
  35.5 0.7 fusion.45
  36.2 0.7 fusion.46
  36.8 1.7 %fusion.62 = (f32[4,1,64,64]{3,2,1,0:T(8,128)}, f32[4,1,64,64]{3,2,1,0:T(8,128)S(1)}, f32[4,1,64,64]{3,2,1,0:T(8,128)S(1)}) fusion(f32[4,3,64,64]{3,2,1,0:T(8,128)} %param.15), kind=kLoop, calls=%fused_computation.110 | loop fusion | bytes 393216 | tf_op jit(solution)/shard_map/slice | solution.py:110
  38.6 0.1 copy.155
  38.7 0.1 copy.156
  38.8 1.0 copy.154
  39.8 1.4 %broadcast_multiply_fusion.2 = (bf16[4,1,64,64]{2,3,1,0:T(8,128)(2,1)}, bf16[4,1,64,64]{2,3,1,0:T(8,128)(2,1)}) fusion(f32[64]{0:T(128)} %copy-done.17, f32[4,1,64,64]{2,3,1,0:T(8,128)S(1)} %copy.154, f32[64,64]{0,1:T(8,128)} %fusion.46), kind=kLoop, calls=%fused_computation.73 | loop fusion | flops 65536 | bytes 147712 | tf_op jit(solution)/shard_map/mul | solution.py:112
  41.2 0.8 broadcast_multiply_fusion.1
  42.0 0.9 pad_maximum_fusion.1
  43.0 0.4 convolution_bitcast_fusion.3
  43.4 2.0 %fusion.63 = (bf16[16,64,128]{2,1,0:T(8,128)(2,1)}, f32[16,64,128]{2,1,0:T(8,128)}) fusion(bf16[2,64,128]{2,1,0:T(8,128)(2,1)} %constant.193, s32[]{:T(128)S(6)} %select_n.46, bf16[16,64,2,32]{1,0,2,3:T(8,128)(2,1)S(1)} %convolution_bitcast_fusion.3), kind=kOutput, calls=%fused_computation.111 | convolution fusion | flops 16908288 | bytes 933892 | tf_op jit(solution)/shard_map/njw,wk->njk/dot_general | solution.py:84
  45.4 0.6 multiply_add_fusion
  46.1 0.1 fusion.39
  46.2 0.2 reduce_window_sum.11
  46.4 0.2 select_reduce_fusion
  46.6 1.8 %convolution_multiply_fusion = bf16[16,64,128]{2,1,0:T(8,128)(2,1)} fusion(bf16[128,128,1]{1,0,2:T(8,128)(2,1)} %constant.189, f32[16,4,64,128]{3,2,0,1:T(8,128)S(1)} %fusion, f32[64]{0:T(128)} %constant.110.clone, f32[16]{0:T(128)} %copy-done.19, f32[16]{0:T(128)} %copy-done.18), kind=kOutput, calls=%fused_computation.7 | convolution fusion | flops 34603008 | bytes 1868160 | tf_op jit(solution)/shard_map/bjk,wk->bjw/dot_general | solution.py:95
  48.4 1.2 %reshape.228 = bf16[16,64,2,64]{3,2,1,0:T(2,128)(2,1)S(1)} reshape(bf16[16,64,128]{2,1,0:T(8,128)(2,1)} %convolution_multiply_fusion) | data formatting | bytes 524288 | tf_op jit(solution)/shard_map/reshape | solution.py:98
  49.6 0.7 copy.120
  50.3 0.4 convolution_bitcast_fusion.1
  50.7 0.7 copy.121
  51.4 0.6 reshape.229
  52.0 1.0 multiply_multiply_fusion.5
  53.3 0.1 add.128
  53.4 0.1 add.129
  53.5 0.1 add.130
  53.7 0.1 mul.373
  54.0 1.0 reduce
  55.0 0.6 reshape.235
  55.6 0.4 fusion.6
  56.1 0.2 copy.137
  56.3 0.8 reshape.236.t_ref
  57.1 0.7 broadcast_in_dim.8.w_ref
  57.8 29.6 %shard_map.139 = f32[16,3,32,128]{3,2,1,0:T(8,128)} custom-call(f32[1536]{0:T(1024)} %reshape.236.t_ref, f32[16,64,128]{2,1,0:T(8,128)} %get-tuple-element.17.r_ref, f32[16,64,128]{2,1,0:T(8,128)} %get-tuple-element.23.q_ref, f32[3,64,128]{2,1,0:T(8,128)} %constant.111.clone.n_ref, f32[64,128]{1,0:T(8,128)} %broadcast_in_dim.8.w_ref), custom_call_target="tpu_custom_call" | custom-call | flops 150994944 | bytes 1048576 | tf_op jit(solution)/shard_map/pallas_call | solution.py:307
  87.4 1.5 %reduce_sum.19 = f32[16,3,32]{2,1,0:T(4,128)S(1)} reduce(f32[16,3,32,128]{3,2,1,0:T(8,128)} %shard_map.139, f32[]{:T(128)} %constant.106.clone.1), dimensions={3}, to_apply=%region_2.3 | reduce | flops 195072 | bytes 792580 | tf_op jit(solution)/shard_map/reduce_sum | solution.py:228
  89.0 0.1 copy.140
  89.1 0.1 reshape.237
  89.3 1.0 fusion.35
  90.2 9.8 %all-to-all-start.1 = ((f32[128,2,13]{2,1,0:T(2,128)}), f32[128,2,13]{2,1,0:T(2,128)S(1)}, u32[]{:S(2)}, u32[]{:S(2)}) async-start(f32[128,2,13]{2,1,0:T(2,128)} %bitcast.31), calls=%async_computation.1 | async-start | bytes 262144 | tf_op jit(solution)/shard_map/all_to_all | solution.py:246
  100.1 9.6 %all-to-all-done.1 = f32[128,2,13]{2,1,0:T(2,128)S(1)} async-done(((f32[128,2,13]{2,1,0:T(2,128)}), f32[128,2,13]{2,1,0:T(2,128)S(1)}, u32[]{:S(2)}, u32[]{:S(2)}) %all-to-all-start.1) | async-done | bytes 13344 | tf_op jit(solution)/shard_map/all_to_all | solution.py:246
  109.6 0.2 slice_reduce_fusion
  109.8 0.3 fusion.28
  110.1 0.1 copy.144
  110.2 0.7 reshape.241
  111.0 0.2 convolution_multiply_fusion.1
  111.2 0.1 reshape.232
  111.3 0.2 constant_dynamic-slice_fusion
  111.5 0.1 copy.160
  111.7 0.3 convolution_bitcast_fusion.4
  112.0 0.8 copy.145
  (73 shorter events, 1.1 us)
Async XLA Ops:
  0.6 52.4 %copy-start = (f32[256,2]{0,1:T(2,128)S(1)}, f32[256,2]{0,1:T(2,128)}, u32[]{:S(2)}) copy-start(f32[256,2]{0,1:T(2,128)} %param.16) | copy-start | bytes 6148
  0.7 2.5 %copy-start.16 = (f32[64]{0:T(128)}, f32[64]{0:T(128)S(1)}, u32[]{:S(2)}) copy-start(f32[64]{0:T(128)S(1)} %get-tuple-element.41) | copy-start | bytes 772
  0.7 2.5 %copy-start.17 = (f32[64]{0:T(128)}, f32[64]{0:T(128)S(1)}, u32[]{:S(2)}) copy-start(f32[64]{0:T(128)S(1)} %get-tuple-element.40) | copy-start | bytes 772
  0.7 2.5 %copy-start.6 = (f32[64,128]{1,0:T(8,128)}, f32[64,128]{1,0:T(8,128)S(1)}, u32[]{:S(2)}) copy-start(f32[64,128]{1,0:T(8,128)S(1)} %fusion.47) | copy-start | bytes 98308
  4.2 4.4 %copy-start.1 = (bf16[64,64,64,1]{2,1,3,0:T(8,128)(2,1)S(1)}, bf16[64,64,64,1]{2,1,3,0:T(8,128)(2,1)}, u32[]{:S(2)}) copy-start(bf16[64,64,64,1]{2,1,3,0:T(8,128)(2,1)} %constant.191) | copy-start | bytes 1572868
  15.4 3.9 %copy-start.20 = (f32[16,2]{0,1:T(2,128)S(1)}, f32[16,2]{0,1:T(2,128)}, u32[]{:S(2)}) copy-start(f32[16,2]{0,1:T(2,128)} %param.14) | copy-start | bytes 388
  15.4 3.9 %copy-start.9 = (bf16[128,128,1,1]{1,0,2,3:T(8,128)(2,1)S(1)}, bf16[128,128,1,1]{1,0,2,3:T(8,128)(2,1)}, u32[]{:S(2)}) copy-start(bf16[128,128,1,1]{1,0,2,3:T(8,128)(2,1)} %constant.190) | copy-start | bytes 98308
  19.4 1.7 %copy-start.18 = (f32[16]{0:T(128)}, f32[16]{0:T(128)S(1)}, u32[]{:S(2)}) copy-start(f32[16]{0:T(128)S(1)} %get-tuple-element.36) | copy-start | bytes 196
  19.4 1.7 %copy-start.19 = (f32[16]{0:T(128)}, f32[16]{0:T(128)S(1)}, u32[]{:S(2)}) copy-start(f32[16]{0:T(128)S(1)} %get-tuple-element.37) | copy-start | bytes 196
  21.1 21.9 %copy-start.4 = (bf16[64,64,64]{2,1,0:T(8,128)(2,1)S(1)}, bf16[64,64,64]{2,1,0:T(8,128)(2,1)}, u32[]{:S(2)}) copy-start(bf16[64,64,64]{2,1,0:T(8,128)(2,1)} %constant.192) | copy-start | bytes 1572868
  23.8 30.2 %all-to-all-start = ((bf16[128,1,64]{2,1,0:T(2,128)(2,1)}), bf16[128,1,64]{2,1,0:T(2,128)(2,1)}, u32[]{:S(2)}, u32[]{:S(2)}) async-start(bf16[128,1,64]{2,1,0:T(2,128)(2,1)} %broadcast_in_dim.7), calls=%async_computation | async-start | bytes 131072 | tf_op jit(solution)/shard_map/all_to_all | solution.py:204
  38.6 6.8 %copy-start.10 = (s32[16,8]{0,1:T(8,128)S(1)}, s32[16,8]{0,1:T(8,128)}, u32[]{:S(2)}) copy-start(s32[16,8]{0,1:T(8,128)} %param.18) | copy-start | bytes 1540
  42.0 3.4 %copy-start.14 = (s32[16,8]{0,1:T(8,128)S(1)}, s32[16,8]{0,1:T(8,128)}, u32[]{:S(2)}) copy-start(s32[16,8]{0,1:T(8,128)} %param.19) | copy-start | bytes 1540
  43.4 6.9 %copy-start.2 = (bf16[64,64,64,1]{2,1,3,0:T(8,128)(2,1)S(1)}, bf16[64,64,64,1]{2,1,3,0:T(8,128)(2,1)}, u32[]{:S(2)}) copy-start(bf16[64,64,64,1]{2,1,3,0:T(8,128)(2,1)} %constant.191) | copy-start | bytes 1572868
  45.4 65.5 %collective-permute-start = (bf16[16,64,128]{2,1,0:T(8,128)(2,1)}, bf16[16,64,128]{2,1,0:T(8,128)(2,1)S(1)}, u32[]{:S(2)}, u32[]{:S(2)}) collective-permute-start(bf16[16,64,128]{2,1,0:T(8,128)(2,1)} %get-tuple-element.38), channel_id=1, source_target_pairs={{0,16},{16,0},{32,48},{48,32},{64,80},{80,64},{96,112},{112,96},{1... | collective-permute-start | bytes 786440 | tf_op jit(solution)/shard_map/ppermute | solution.py:23
  50.7 1.3 %copy-start.7 = (f32[64,128]{1,0:T(8,128)S(1)}, f32[64,128]{1,0:T(8,128)}, u32[]{:S(2)}) copy-start(f32[64,128]{1,0:T(8,128)} %copy-done.6) | copy-start | bytes 98308
  50.7 2.4 %copy-start.12 = (s32[16,8]{0,1:T(8,128)S(1)}, s32[16,8]{0,1:T(8,128)}, u32[]{:S(2)}) copy-start(s32[16,8]{0,1:T(8,128)} %get-tuple-element.32) | copy-start | bytes 1540
  50.7 2.6 %copy-start.13 = (f32[3,16,8]{1,2,0:T(8,128)S(1)}, f32[3,16,8]{1,2,0:T(8,128)}, u32[]{:S(2)}) copy-start(f32[3,16,8]{1,2,0:T(8,128)} %param.17) | copy-start | bytes 4612
  51.4 2.3 %copy-start.15 = (f32[3,4]{1,0:T(4,128)S(1)}, f32[3,4]{1,0:T(4,128)}, u32[]{:S(2)}) copy-start(f32[3,4]{1,0:T(4,128)} %constant.121) | copy-start | bytes 148
  51.4 2.4 %copy-start.11 = (f32[16,8]{0,1:T(8,128)S(1)}, f32[16,8]{0,1:T(8,128)}, u32[]{:S(2)}) copy-start(f32[16,8]{0,1:T(8,128)} %get-tuple-element.33) | copy-start | bytes 1540
  52.0 5.1 %copy-start.21 = (f32[64]{0:T(128)S(1)}, f32[64]{0:T(128)}, u32[]{:S(2)}) copy-start(f32[64]{0:T(128)} %constant.110.clone) | copy-start | bytes 772
  87.4 23.5 %copy-start.3 = (f32[16,64,128]{2,1,0:T(8,128)S(1)}, f32[16,64,128]{2,1,0:T(8,128)}, u32[]{:S(2)}) copy-start(f32[16,64,128]{2,1,0:T(8,128)} %get-tuple-element.39) | copy-start | bytes 1572868
  87.4 23.6 %copy-start.22 = (bf16[128,128,1]{1,0,2:T(8,128)(2,1)S(1)}, bf16[128,128,1]{1,0,2:T(8,128)(2,1)}, u32[]{:S(2)}) copy-start(bf16[128,128,1]{1,0,2:T(8,128)(2,1)} %constant.189) | copy-start | bytes 98308
  87.4 24.3 %copy-start.5 = (bf16[64,64,64]{2,1,0:T(8,128)(2,1)S(1)}, bf16[64,64,64]{2,1,0:T(8,128)(2,1)}, u32[]{:S(2)}) copy-start(bf16[64,64,64]{2,1,0:T(8,128)(2,1)} %constant.192) | copy-start | bytes 1572868
  89.1 22.8 %copy-start.8 = (f32[64,64]{0,1:T(8,128)S(1)}, f32[64,64]{0,1:T(8,128)}, u32[]{:S(2)}) copy-start(f32[64,64]{0,1:T(8,128)} %fusion.46) | copy-start | bytes 49156
  90.2 19.4 %all-to-all-start.1 = ((f32[128,2,13]{2,1,0:T(2,128)}), f32[128,2,13]{2,1,0:T(2,128)S(1)}, u32[]{:S(2)}, u32[]{:S(2)}) async-start(f32[128,2,13]{2,1,0:T(2,128)} %bitcast.31), calls=%async_computation.1 | async-start | bytes 262144 | tf_op jit(solution)/shard_map/all_to_all | solution.py:246

commit v3 on v0

--- a/solution.py
+++ b/solution.py
@@ -9,6 +9,7 @@
 from jax.sharding import PartitionSpec as P
 
 HIGH = lax.Precision.HIGHEST
+SPECTRAL = lax.Precision.DEFAULT
 SOFTENING = 0.04
 
 
@@ -75,7 +76,7 @@
     batch_size, degrees, coef_width = coeff.shape
     orders = legendre.shape[0]
     parted = coeff.reshape(batch_size, degrees, 2, orders)
-    return jnp.einsum("mjl,nlcm->njcm", legendre, parted, precision=HIGH)
+    return jnp.einsum("mjl,nlcm->njcm", legendre, parted, precision=SPECTRAL)
 
 
 def fourier_synth(partial_legendre, fourier_rows):
@@ -84,14 +85,14 @@
         "njw,wk->njk",
         partial_legendre.reshape(batch_size, nlat, two * orders),
         fourier_rows,
-        precision=HIGH,
+        precision=SPECTRAL,
     )
 
 
 def analysis_fourier(traction_grid, fourier, quad_weight):
     batch_size, nlat, nlon = traction_grid.shape
     projected = (
-        jnp.einsum("bjk,wk->bjw", traction_grid, fourier, precision=HIGH)
+        jnp.einsum("bjk,wk->bjw", traction_grid, fourier, precision=SPECTRAL)
         * quad_weight[None, :, None]
     )
     return projected.reshape(batch_size, nlat, 2, fourier.shape[0] // 2)
@@ -99,7 +100,7 @@
 
 def analysis_legendre(coef_grid, legendre):
     batch_size = coef_grid.shape[0]
-    result = jnp.einsum("mjl,bjcm->blcm", legendre, coef_grid, precision=HIGH)
+    result = jnp.einsum("mjl,bjcm->blcm", legendre, coef_grid, precision=SPECTRAL)
     return result.reshape(batch_size, legendre.shape[2], 2 * legendre.shape[0])
 
 
@@ -157,15 +158,27 @@
         jnp.float32
     )
     prepared = prepare(coeffs, keep_mask)
+    point_lat = np.arange(nlat // 4, nlat, nlat // 2)
+    point_lon = np.arange(0, nlon, nlon // 2)
+    point_legendre = legendre[:, point_lat, :]
+    point_partial = jnp.einsum(
+        "mjl,nlcm->njcm",
+        point_legendre,
+        prepared[:, 0].reshape(drop_count, degrees, 2, degrees),
+        precision=HIGH,
+    )
+    point_surface = jnp.einsum(
+        "njw,wk->njk",
+        point_partial.reshape(drop_count, point_lat.size, coef_width),
+        fourier[:, point_lon],
+        precision=HIGH,
+    )
+    own_points = jnp.exp(point_surface).astype(jnp.bfloat16).reshape(drop_count, -1)
     partial_legendre = legendre_synth(
         prepared.reshape(drop_count * 4, degrees, coef_width), legendre
     )
     surface = fourier_synth(partial_legendre, fourier).reshape(drop_count, 4, nlat, nlon)
     radius, traction_grid = traction(surface, material)
-    traction_coeffs = (
-        analysis_legendre(analysis_fourier(traction_grid, fourier, quad_weight), legendre)
-        * keep_mask
-    )
     split_count = split_coeffs.shape[0]
     half_width = split_coeffs.shape[3]
     half_orders = half_width // 2
@@ -191,15 +204,12 @@
     split_radius, split_grid = traction(
         split_surface.reshape(split_count, 4, nlat, nlon), own_material
     )
-    coef_grid = analysis_fourier(split_grid, fourier, quad_weight)
-    own_grid = lax.dynamic_slice_in_dim(coef_grid, half_index * half_orders, half_orders, 3)
-    split_traction = analysis_legendre(own_grid, own_legendre) * keep_half[None]
     near_grid = jnp.stack([radius, traction_grid], axis=1).astype(jnp.bfloat16)
-    point_grid = near_grid[:, 0, nlat // 4 :: nlat // 2, :: nlon // 2]
-    point_count = point_grid.shape[1] * point_grid.shape[2]
-    own_points = point_grid.reshape(drop_count, point_count)
+    point_lat = np.arange(nlat // 4, nlat, nlat // 2)
+    point_lon = np.arange(0, nlon, nlon // 2)
+    point_count = point_lat.size * point_lon.size
     target_normal = normals[:, nlat // 4 :: nlat // 2, :: nlon // 2].reshape(3, point_count)
-    all_points = lax.all_gather(own_points, ("row", "col"), axis=0, tiled=True)
+    all_points = gather_all(own_points.reshape(-1)).reshape(-1, point_count)
     total_drops = all_points.shape[0]
     readers = reader_dev.shape[1]
     target = (reader_dev * drop_count + reader_slot).reshape(-1)
@@ -217,14 +227,67 @@
     source_traction = near_grid[:, 1].astype(jnp.float32)
     cell_weight = jnp.broadcast_to(quad_weight[:, None], (nlat, nlon))
     partial = near_field(target_point, source_radius, source_traction, normals, cell_weight)
+    partial, traction_grid, split_grid = lax.optimization_barrier(
+        (partial, traction_grid, split_grid)
+    )
     contribution = jnp.sum(partial, axis=3) / (8.0 * math.pi)
     contribution = jnp.transpose(
         contribution.reshape(drop_count, 3, readers, point_count), (0, 2, 1, 3)
     ).reshape(drop_count * readers, 3 * point_count)
     dense = jnp.dot(jnp.transpose(pick), contribution, precision=HIGH)
-    mine = lax.psum_scatter(dense, ("row", "col"), scatter_dimension=0, tiled=True)
+    mine = reduce_to_owner(dense.reshape(-1, drop_count * 3 * point_count))
     near_velocity = jnp.transpose(mine.reshape(drop_count, 3, point_count), (1, 0, 2))
+    traction_coeffs = (
+        analysis_legendre(analysis_fourier(traction_grid, fourier, quad_weight), legendre)
+        * keep_mask
+    )
+    coef_grid = analysis_fourier(split_grid, fourier, quad_weight)
+    own_grid = lax.dynamic_slice_in_dim(coef_grid, half_index * half_orders, half_orders, 3)
+    split_traction = analysis_legendre(own_grid, own_legendre) * keep_half[None]
     return (traction_coeffs, split_traction, near_velocity.reshape(3, drop_count * point_count))
+
+
+def index_bits():
+    bits = []
+    for axis in ("row", "col"):
+        size = lax.axis_size(axis)
+        width = size.bit_length() - 1
+        assert 1 << width == size
+        bits += [(axis, k) for k in reversed(range(width))]
+    return bits
+
+
+def exchange_order(bits):
+    return sorted(bits, key=lambda item: (item[0] != "row", item[1]))
+
+
+def gather_all(own):
+    bits = index_bits()
+    done = []
+    buf = own
+    for axis, k in exchange_order(bits):
+        other = from_partner(buf, axis, k)
+        upper = (lax.axis_index(axis) >> k) & 1
+        buf = jnp.where(upper == 1, jnp.stack([other, buf]), jnp.stack([buf, other]))
+        done.insert(0, (axis, k))
+    buf = jnp.transpose(buf, [done.index(item) for item in bits] + [len(bits)])
+    return buf.reshape((-1,) + own.shape)
+
+
+def reduce_to_owner(dense):
+    bits = index_bits()
+    left = list(bits)
+    buf = dense.reshape((2,) * len(bits) + dense.shape[1:])
+    for axis, k in exchange_order(bits):
+        place = left.index((axis, k))
+        lower = lax.index_in_dim(buf, 0, place, keepdims=False)
+        upper_half = lax.index_in_dim(buf, 1, place, keepdims=False)
+        upper = (lax.axis_index(axis) >> k) & 1
+        keep = jnp.where(upper == 1, upper_half, lower)
+        send = jnp.where(upper == 1, lower, upper_half)
+        buf = keep + from_partner(send, axis, k)
+        left.pop(place)
+    return buf
 
 
 def near_kernel(t_ref, r_ref, q_ref, n_ref, w_ref, o_ref, s_ref):

time: 799 us -> 127 us (0.16)
  waiting for transfers between devices: 627 us -> 19.2 us
  blocking collectives: 58 us -> 0 us
  starting transfers between devices: 0.04 us -> 31.5 us
  between operations: 14.4 us -> 1.53 us
  matrix products: 25 us -> 14 us
  local copies, waits for them, and re-layouts: 36.5 us -> 26 us
    reduce_scatter x1 -> x0, waiting for transfers between devices: 627 us -> none  [per_device(): lax.psum_scatter(dense, ('row', 'col'), scatter_dimension=0, tiled=True)]
    all_gather x1 -> x0, blocking collectives: 58 us -> none  [per_device(): all_points = lax.all_gather(own_points, ('row', 'col'), axis=0, tiled=True)]
    ppermute x1 -> x15, starting transfers between devices: 0.01 us -> 31.5 us  [from_partner(): return lax.ppermute(block, axis, route)]
    ppermute x1 -> x15, waiting for transfers between devices: 0.01 us -> 19.2 us  [from_partner(): return lax.ppermute(block, axis, route)]
    dot_general x6 -> x8, matrix products: 17.5 us -> 11.3 us  [the longest x1 7.38 us: per_device(): jnp.einsum('mjl,nlcm->njcm', point_legendre, prepared[:, 0].reshape(drop_...]
  transfers between devices with their start and end apart: 2 -> 15, of which waited for: 1 -> 13; matrix products, arithmetic and copies ran while one was open for 2% -> 23% of each run, Pallas kernels for 0% -> 23%
where the time goes in v3:
time: 127 us
  starting transfers between devices  31.5 us (25%)
  Pallas kernels  29.7 us (23%)
  local copies, waits for them, and re-layouts  26 us (20%)
  waiting for transfers between devices  19.2 us (15%)
  matrix products  14 us (11%)
  other arithmetic  5.35 us (4%)
  between operations  1.53 us (1%)
    ppermute x15, starting transfers between devices, from_partner(): return lax.ppermute(block, axis, route)  31.5 us
    pallas_call x1, Pallas kernels, near_field(): pl.pallas_call(near_kernel, grid=(drops,), in_specs=[pl.BlockSpec(memory_...  29.7 us
    ppermute x15, waiting for transfers between devices, from_partner(): return lax.ppermute(block, axis, route)  19.2 us
    dot_general x1, matrix products, per_device(): jnp.einsum('mjl,nlcm->njcm', point_legendre, prepared[:, 0].reshape(drop_...  7.38 us
    another operation x2, local copies, waits for them, and re-layouts, legendre_synth(): parted = coeff.reshape(batch_size, degrees, 2, orders)  5.24 us
    transpose x1, local copies, waits for them, and re-layouts, legendre_synth(): return jnp.einsum('mjl,nlcm->njcm', legendre, parted, precision=SPECTRAL)  4.59 us
    dot_general x1, local copies, waits for them, and re-layouts, fourier_synth(): jnp.einsum('njw,wk->njk', partial_legendre.reshape(batch_size, nlat, two...  3.9 us
    dot_general x2, matrix products, legendre_synth(): return jnp.einsum('mjl,nlcm->njcm', legendre, parted, precision=SPECTRAL)  2.69 us
  transfers between devices with their start and end apart: 15, of which 13 were waited for; matrix products, arithmetic and copies ran while one was open for 23% of the time, Pallas kernels for 23%

profile of v3, /device:TPU:0, one launch (start us, length us, event | category | flops | bytes accessed | tf_op | source)
XLA Modules:
  0.0 127.1 jit_solution(11334618626475210482)
XLA Ops:
  0.7 1.1 slice.104
  1.8 0.6 squeeze.14
  2.4 0.7 copy.138
  3.4 7.4 %convolution_bitcast_fusion.4 = f32[16,2,2,64]{0,1,2,3:T(2,128)S(1)} fusion(f32[64,2,64,1]{2,1,3,0:T(2,128)S(1)} %copy-done.10, f32[16,64,2,64]{1,0,2,3:T(8,128)S(1)} %copy.138, f32[16,64]{1,0:T(8,128)S(1)} %fusion.49, f32[64,2,64]{0,1,2:T(2,128)S(1)} %compare_convert_fusion), kind=kOutput, calls=%fused_computation.9 | convolution fusion | flops 3407872 | bytes 610304 | tf_op jit(solution)/shard_map/mjl,nlcm->njcm/dot_general | solution.py:164
  11.0 0.6 gather_fusion
  11.6 0.2 fusion.2
  12.9 0.4 convolution_bitcast_fusion.3
  13.3 1.2 fusion.64
  14.4 0.5 collective-permute-start.7
  15.2 0.3 broadcast_multiply_fusion
  15.6 0.8 reshape_reshape.17
  16.5 4.4 %copy.146 = bf16[64,64,2,64]{1,0,2,3:T(8,128)(2,1)} copy(bf16[64,64,2,64]{3,2,1,0:T(2,128)(2,1)S(1)} %reshape_reshape.17) | data formatting | bytes 2097152 | tf_op jit(solution)/shard_map/reshape;reshape | solution.py:78
  20.9 2.3 %convolution_bitcast_fusion = bf16[64,64,2,64]{1,0,2,3:T(8,128)(2,1)S(1)} fusion(bf16[64,64,2,64]{1,0,2,3:T(8,128)(2,1)} %copy.146, bf16[64,64,64,1]{2,1,3,0:T(8,128)(2,1)S(1)} %copy-done.1), kind=kOutput, calls=%fused_computation.1 | convolution fusion | flops 67108864 | bytes 2621440 | tf_op jit(solution)/shard_map/mjl,nlcm->njcm/dot_general | solution.py:79
  23.2 4.6 %copy.147 = bf16[64,64,2,64]{3,2,1,0:T(2,128)(2,1)} copy(bf16[64,64,2,64]{1,0,2,3:T(8,128)(2,1)S(1)} %convolution_bitcast_fusion) | data formatting | bytes 2097152 | tf_op jit(solution)/shard_map/mjl,nlcm->njcm/transpose | solution.py:79
  27.8 3.9 %dot_general.42 = bf16[16,4,64,128]{3,2,1,0:T(8,128)(2,1)S(1)} reshape(bf16[64,64,2,64]{3,2,1,0:T(2,128)(2,1)} %copy.147) | data formatting | bytes 2097152 | tf_op jit(solution)/shard_map/njw,wk->njk/dot_general | solution.py:84
  31.7 0.4 fusion
  32.2 1.1 bitcast_convert_fusion
  33.3 0.2 fusion.15
  34.5 2.1 %collective-permute-start.1 = (bf16[2,64]{1,0:T(2,128)(2,1)S(1)}, bf16[2,64]{1,0:T(2,128)(2,1)S(1)}, u32[]{:S(2)}, u32[]{:S(2)}) collective-permute-start(bf16[2,64]{1,0:T(2,128)(2,1)S(1)} %broadcast_select_fusion.17), channel_id=1, source_target_pairs={{0,32},{32,0},{16,48},{48,16},{64,96},{96,64},{80,112},{112,80},{1... | collective-permute-start | bytes 776 | tf_op jit(solution)/shard_map/ppermute | solution.py:23
  36.6 1.5 %collective-permute-done.1 = bf16[2,64]{1,0:T(2,128)(2,1)S(1)} collective-permute-done((bf16[2,64]{1,0:T(2,128)(2,1)S(1)}, bf16[2,64]{1,0:T(2,128)(2,1)S(1)}, u32[]{:S(2)}, u32[]{:S(2)}) %collective-permute-start.1) | collective-permute-done | bytes 288 | tf_op jit(solution)/shard_map/ppermute | solution.py:23
  38.1 4.1 %collective-permute-start.2 = (bf16[2,2,64]{2,1,0:T(2,128)(2,1)S(1)}, bf16[2,2,64]{2,1,0:T(2,128)(2,1)S(1)}, u32[]{:S(2)}, u32[]{:S(2)}) collective-permute-start(bf16[2,2,64]{2,1,0:T(2,128)(2,1)S(1)} %broadcast_select_fusion.15), channel_id=1, source_target_pairs={{0,64},{64,0},{16,80},{80,16},{32,96},{96,32},{48,112},{112,48},{1... | collective-permute-start | bytes 1544 | tf_op jit(solution)/shard_map/ppermute | solution.py:23
  42.2 1.5 %collective-permute-done.2 = bf16[2,2,64]{2,1,0:T(2,128)(2,1)S(1)} collective-permute-done((bf16[2,2,64]{2,1,0:T(2,128)(2,1)S(1)}, bf16[2,2,64]{2,1,0:T(2,128)(2,1)S(1)}, u32[]{:S(2)}, u32[]{:S(2)}) %collective-permute-start.2) | collective-permute-done | bytes 544 | tf_op jit(solution)/shard_map/ppermute | solution.py:23
  43.7 1.6 %collective-permute-start.3 = (bf16[2,2,2,64]{3,2,1,0:T(2,128)(2,1)S(1)}, bf16[2,2,2,64]{3,2,1,0:T(2,128)(2,1)S(1)}, u32[]{:S(2)}, u32[]{:S(2)}) collective-permute-start(bf16[2,2,2,64]{3,2,1,0:T(2,128)(2,1)S(1)} %broadcast_select_fusion.11), channel_id=1, source_target_pairs={{0,1},{1,0},{2,3},{3,2},{4,5},{5,4},{6,7},{7,6},{8,9},{9,8},{10,11... | collective-permute-start | bytes 3080 | tf_op jit(solution)/shard_map/ppermute | solution.py:23
  45.4 2.1 %collective-permute-done.3 = bf16[2,2,2,64]{3,2,1,0:T(2,128)(2,1)S(1)} collective-permute-done((bf16[2,2,2,64]{3,2,1,0:T(2,128)(2,1)S(1)}, bf16[2,2,2,64]{3,2,1,0:T(2,128)(2,1)S(1)}, u32[]{:S(2)}, u32[]{:S(2)}) %collective-permute-start.3) | collective-permute-done | bytes 1056 | tf_op jit(solution)/shard_map/ppermute | solution.py:23
  47.4 3.3 %collective-permute-start.4 = (bf16[2,2,2,2,64]{4,3,2,1,0:T(2,128)(2,1)S(1)}, bf16[2,2,2,2,64]{4,3,2,1,0:T(2,128)(2,1)S(1)}, u32[]{:S(2)}, u32[]{:S(2)}) collective-permute-start(bf16[2,2,2,2,64]{4,3,2,1,0:T(2,128)(2,1)S(1)} %broadcast_select_fusion.8), channel_id=1, source_target_pairs={{0,2},{2,0},{1,3},{3,1},{4,6},{6,4},{5,7},{7,5},{8,10},{10,8},{9,1... | collective-permute-start | bytes 6152 | tf_op jit(solution)/shard_map/ppermute | solution.py:23
  50.8 2.0 %collective-permute-done.4 = bf16[2,2,2,2,64]{4,3,2,1,0:T(2,128)(2,1)S(1)} collective-permute-done((bf16[2,2,2,2,64]{4,3,2,1,0:T(2,128)(2,1)S(1)}, bf16[2,2,2,2,64]{4,3,2,1,0:T(2,128)(2,1)S(1)}, u32[]{:S(2)}, u32[]{:S(2)}) %collective-permute-start.4) | collective-permute-done | bytes 2080 | tf_op jit(solution)/shard_map/ppermute | solution.py:23
  52.8 1.7 %collective-permute-start.5 = (bf16[2,2,2,2,2,64]{5,4,3,2,1,0:T(2,128)(2,1)S(1)}, bf16[2,2,2,2,2,64]{5,4,3,2,1,0:T(2,128)(2,1)S(1)}, u32[]{:S(2)}, u32[]{:S(2)}) collective-permute-start(bf16[2,2,2,2,2,64]{5,4,3,2,1,0:T(2,128)(2,1)S(1)} %broadcast_select_fusion.5), channel_id=1, source_target_pairs={{0,4},{4,0},{1,5},{5,1},{2,6},{6,2},{3,7},{7,3},{8,12},{12,8},{9,1... | collective-permute-start | bytes 12296 | tf_op jit(solution)/shard_map/ppermute | solution.py:23
  54.5 2.0 %collective-permute-done.5 = bf16[2,2,2,2,2,64]{5,4,3,2,1,0:T(2,128)(2,1)S(1)} collective-permute-done((bf16[2,2,2,2,2,64]{5,4,3,2,1,0:T(2,128)(2,1)S(1)}, bf16[2,2,2,2,2,64]{5,4,3,2,1,0:T(2,128)(2,1)S(1)}, u32[]{:S(2)}, u32[]{:S(2)}) %collective-permute-start.5) | collective-permute-done | bytes 4128 | tf_op jit(solution)/shard_map/ppermute | solution.py:23
  56.6 3.3 %collective-permute-start.6 = (bf16[2,2,2,2,2,2,64]{6,5,4,3,2,1,0:T(2,128)(2,1)S(1)}, bf16[2,2,2,2,2,2,64]{6,5,4,3,2,1,0:T(2,128)(2,1)S(1)}, u32[]{:S(2)}, u32[]{:S(2)}) collective-permute-start(bf16[2,2,2,2,2,2,64]{6,5,4,3,2,1,0:T(2,128)(2,1)S(1)} %broadcast_select_fusion.2), channel_id=1, source_target_pairs={{0,8},{8,0},{1,9},{9,1},{2,10},{10,2},{3,11},{11,3},{4,12},{12,4},... | collective-permute-start | bytes 24584 | tf_op jit(solution)/shard_map/ppermute | solution.py:23
  59.9 2.0 %collective-permute-done.6 = bf16[2,2,2,2,2,2,64]{6,5,4,3,2,1,0:T(2,128)(2,1)S(1)} collective-permute-done((bf16[2,2,2,2,2,2,64]{6,5,4,3,2,1,0:T(2,128)(2,1)S(1)}, bf16[2,2,2,2,2,2,64]{6,5,4,3,2,1,0:T(2,128)(2,1)S(1)}, u32[]{:S(2)}, u32[]{:S(2)}) %collective-permute-start.6) | collective-permute-done | bytes 8224 | tf_op jit(solution)/shard_map/ppermute | solution.py:23
  62.0 0.6 reshape_reshape.16
  62.6 0.4 fusion.10
  63.1 0.2 copy.145
  63.3 0.8 reshape.870.t_ref
  64.1 0.7 broadcast_in_dim.8.w_ref
  64.8 29.7 %shard_map.175 = f32[16,3,32,128]{3,2,1,0:T(8,128)} custom-call(f32[1536]{0:T(1024)} %reshape.870.t_ref, f32[16,64,128]{2,1,0:T(8,128)} %get-tuple-element.23.r_ref, f32[16,64,128]{2,1,0:T(8,128)} %get-tuple-element.22.q_ref, f32[3,64,128]{2,1,0:T(8,128)} %constant.120.clone.n_ref, f32[64,128]{1,0:T(8,128)} %broadcast_in_dim.8.w_ref), custom_call_target="tpu_custom_call" | custom-call | flops 150994944 | bytes 1048576 | tf_op jit(solution)/shard_map/pallas_call | solution.py:339
  94.5 1.1 convert_add_fusion
  95.7 0.3 reduce_sum.9
  96.3 0.7 fusion.17
  97.0 0.6 reshape_reshape.19
  97.7 0.2 convolution_multiply_fusion
  98.0 0.2 reshape.873
  98.2 0.7 copy.160
  99.0 1.6 %collective-permute-start.9 = (f32[2,2,2,2,2,192]{5,4,3,2,1,0:T(2,128)S(1)}, f32[2,2,2,2,2,192]{5,4,3,2,1,0:T(2,128)S(1)}, u32[]{:S(2)}, u32[]{:S(2)}) collective-permute-start(f32[2,2,2,2,2,192]{5,4,3,2,1,0:T(2,128)S(1)} %fusion.36), channel_id=1, source_target_pairs={{0,32},{32,0},{16,48},{48,16},{64,96},{96,64},{80,112},{112,80},{1... | collective-permute-start | bytes 73736 | tf_op jit(solution)/shard_map/ppermute | solution.py:23
  100.7 0.4 convolution_bitcast_fusion.1
  101.1 0.7 copy.161
  101.8 0.6 reshape.874
  102.4 0.7 collective-permute-done.9
  103.1 3.6 %collective-permute-start.10 = (f32[2,2,2,2,192]{4,3,2,1,0:T(2,128)S(1)}, f32[2,2,2,2,192]{4,3,2,1,0:T(2,128)S(1)}, u32[]{:S(2)}, u32[]{:S(2)}) collective-permute-start(f32[2,2,2,2,192]{4,3,2,1,0:T(2,128)S(1)} %select_bitcast_fusion), channel_id=1, source_target_pairs={{0,64},{64,0},{16,80},{80,16},{32,96},{96,32},{48,112},{112,48},{1... | collective-permute-start | bytes 36872 | tf_op jit(solution)/shard_map/ppermute | solution.py:23
  106.7 1.0 multiply_multiply_fusion.5
  107.7 0.7 collective-permute-done.10
  108.5 1.6 %collective-permute-start.11 = (f32[2,2,2,192]{3,2,1,0:T(2,128)S(1)}, f32[2,2,2,192]{3,2,1,0:T(2,128)S(1)}, u32[]{:S(2)}, u32[]{:S(2)}) collective-permute-start(f32[2,2,2,192]{3,2,1,0:T(2,128)S(1)} %bitcast.226), channel_id=1, source_target_pairs={{0,1},{1,0},{2,3},{3,2},{4,5},{5,4},{6,7},{7,6},{8,9},{9,8},{10,11... | collective-permute-start | bytes 18440 | tf_op jit(solution)/shard_map/ppermute | solution.py:23
  110.0 0.2 convolution_multiply_fusion.1
  110.3 1.9 %collective-permute-done.11 = f32[2,2,2,192]{3,2,1,0:T(2,128)S(1)} collective-permute-done((f32[2,2,2,192]{3,2,1,0:T(2,128)S(1)}, f32[2,2,2,192]{3,2,1,0:T(2,128)S(1)}, u32[]{:S(2)}, u32[]{:S(2)}) %collective-permute-start.11) | collective-permute-done | bytes 6176 | tf_op jit(solution)/shard_map/ppermute | solution.py:23
  112.2 3.1 %collective-permute-start.12 = (f32[2,2,192]{2,1,0:T(2,128)S(1)}, f32[2,2,192]{2,1,0:T(2,128)S(1)}, u32[]{:S(2)}, u32[]{:S(2)}) collective-permute-start(f32[2,2,192]{2,1,0:T(2,128)S(1)} %bitcast.233), channel_id=1, source_target_pairs={{0,2},{2,0},{1,3},{3,1},{4,6},{6,4},{5,7},{7,5},{8,10},{10,8},{9,1... | collective-permute-start | bytes 9224 | tf_op jit(solution)/shard_map/ppermute | solution.py:23
  115.4 0.2 constant_dynamic-slice_fusion
  115.7 1.7 %collective-permute-done.12 = f32[2,2,192]{2,1,0:T(2,128)S(1)} collective-permute-done((f32[2,2,192]{2,1,0:T(2,128)S(1)}, f32[2,2,192]{2,1,0:T(2,128)S(1)}, u32[]{:S(2)}, u32[]{:S(2)}) %collective-permute-start.12) | collective-permute-done | bytes 3104 | tf_op jit(solution)/shard_map/ppermute | solution.py:23
  117.5 1.7 %collective-permute-start.13 = (f32[2,192]{1,0:T(2,128)S(1)}, f32[2,192]{1,0:T(2,128)S(1)}, u32[]{:S(2)}, u32[]{:S(2)}) collective-permute-start(f32[2,192]{1,0:T(2,128)S(1)} %bitcast.235), channel_id=1, source_target_pairs={{0,4},{4,0},{1,5},{5,1},{2,6},{6,2},{3,7},{7,3},{8,12},{12,8},{9,1... | collective-permute-start | bytes 4616 | tf_op jit(solution)/shard_map/ppermute | solution.py:23
  119.1 0.2 convolution_bitcast_fusion.5
  119.4 1.7 %collective-permute-done.13 = f32[2,192]{1,0:T(2,128)S(1)} collective-permute-done((f32[2,192]{1,0:T(2,128)S(1)}, f32[2,192]{1,0:T(2,128)S(1)}, u32[]{:S(2)}, u32[]{:S(2)}) %collective-permute-start.13) | collective-permute-done | bytes 1568 | tf_op jit(solution)/shard_map/ppermute | solution.py:23
  121.1 3.3 %collective-permute-start.14 = (f32[192]{0:T(256)S(1)}, f32[192]{0:T(256)S(1)}, u32[]{:S(2)}, u32[]{:S(2)}) collective-permute-start(f32[192]{0:T(256)S(1)} %bitcast.236), channel_id=1, source_target_pairs={{0,8},{8,0},{1,9},{9,1},{2,10},{10,2},{3,11},{11,3},{4,12},{12,4},... | collective-permute-start | bytes 2312 | tf_op jit(solution)/shard_map/ppermute | solution.py:23
  124.4 0.8 copy.189
  125.2 1.1 collective-permute-done.14
  126.4 0.7 reshape.879
  (131 shorter events, 4.2 us)
Async XLA Ops:
  0.6 33.5 %copy-start = (f32[256,2]{0,1:T(2,128)S(1)}, f32[256,2]{0,1:T(2,128)}, u32[]{:S(2)}) copy-start(f32[256,2]{0,1:T(2,128)} %param.20) | copy-start | bytes 6148
  0.7 2.5 %copy-start.19 = (s32[16]{0:T(128)S(1)}, s32[16]{0:T(128)}, u32[]{:S(2)}) copy-start(s32[16]{0:T(128)} %param.17) | copy-start | bytes 196
  1.8 1.6 %copy-start.10 = (f32[64,2,64,1]{2,1,3,0:T(2,128)S(1)}, f32[64,2,64,1]{2,1,3,0:T(2,128)}, u32[]{:S(2)}) copy-start(f32[64,2,64,1]{2,1,3,0:T(2,128)} %constant.136) | copy-start | bytes 98308
  2.4 8.6 %copy-start.2 = (f32[128,128]{0,1:T(8,128)S(1)}, f32[128,128]{0,1:T(8,128)}, u32[]{:S(2)}) copy-start(f32[128,128]{0,1:T(8,128)} %constant.118.clone) | copy-start | bytes 196612
  3.2 9.2 %copy-start.8 = (f32[4,3,64,64]{3,2,1,0:T(8,128)S(1)}, f32[4,3,64,64]{3,2,1,0:T(8,128)}, u32[]{:S(2)}) copy-start(f32[4,3,64,64]{3,2,1,0:T(8,128)} %param.19) | copy-start | bytes 589828
  10.8 2.1 %copy-start.5 = (bf16[64,64,64]{2,1,0:T(8,128)(2,1)S(1)}, bf16[64,64,64]{2,1,0:T(8,128)(2,1)}, u32[]{:S(2)}) copy-start(bf16[64,64,64]{2,1,0:T(8,128)(2,1)} %constant.248) | copy-start | bytes 1572868
  11.6 1.7 %copy-start.13 = (bf16[2,64,128]{2,1,0:T(8,128)(2,1)S(1)}, bf16[2,64,128]{2,1,0:T(8,128)(2,1)}, u32[]{:S(2)}) copy-start(bf16[2,64,128]{2,1,0:T(8,128)(2,1)} %constant.249) | copy-start | bytes 98308
  12.1 22.4 %collective-permute-start = (bf16[64]{0:T(256)(128)(2,1)S(1)}, bf16[64]{0:T(256)(128)(2,1)S(1)}, u32[]{:S(2)}, u32[]{:S(2)}) collective-permute-start(bf16[64]{0:T(256)(128)(2,1)S(1)} %reshape_reshape.15), channel_id=1, source_target_pairs={{0,16},{16,0},{32,48},{48,32},{64,80},{80,64},{96,112},{112,96},{1... | collective-permute-start | bytes 392 | tf_op jit(solution)/shard_map/ppermute | solution.py:23
  12.4 2.8 %copy-start.3 = (f32[16,3,64,128]{3,2,1,0:T(8,128)S(1)}, f32[16,3,64,128]{3,2,1,0:T(8,128)}, u32[]{:S(2)}) copy-start(f32[16,3,64,128]{3,2,1,0:T(8,128)} %param.16) | copy-start | bytes 4718596
  14.4 80.0 %collective-permute-start.7 = (bf16[16,64,128]{2,1,0:T(8,128)(2,1)}, bf16[16,64,128]{2,1,0:T(8,128)(2,1)}, u32[]{:S(2)}, u32[]{:S(2)}) collective-permute-start(bf16[16,64,128]{2,1,0:T(8,128)(2,1)} %get-tuple-element.46), channel_id=1, source_target_pairs={{0,16},{16,0},{32,48},{48,32},{64,80},{80,64},{96,112},{112,96},{1... | collective-permute-start | bytes 786440 | tf_op jit(solution)/shard_map/ppermute | solution.py:23
  16.5 4.4 %copy-start.1 = (bf16[64,64,64,1]{2,1,3,0:T(8,128)(2,1)S(1)}, bf16[64,64,64,1]{2,1,3,0:T(8,128)(2,1)}, u32[]{:S(2)}) copy-start(bf16[64,64,64,1]{2,1,3,0:T(8,128)(2,1)} %constant.247) | copy-start | bytes 1572868
  27.8 3.9 %copy-start.18 = (f32[16,2]{0,1:T(2,128)S(1)}, f32[16,2]{0,1:T(2,128)}, u32[]{:S(2)}) copy-start(f32[16,2]{0,1:T(2,128)} %param.18) | copy-start | bytes 388
  27.8 3.9 %copy-start.11 = (bf16[128,128,1,1]{0,1,2,3:T(8,128)(2,1)S(1)}, bf16[128,128,1,1]{0,1,2,3:T(8,128)(2,1)}, u32[]{:S(2)}) copy-start(bf16[128,128,1,1]{0,1,2,3:T(8,128)(2,1)} %constant.246) | copy-start | bytes 98308
  32.2 1.4 %copy-start.12 = (f32[3,16,8]{1,2,0:T(8,128)S(1)}, f32[3,16,8]{1,2,0:T(8,128)}, u32[]{:S(2)}) copy-start(f32[3,16,8]{1,2,0:T(8,128)} %param.21) | copy-start | bytes 4612
  32.2 1.8 %copy-start.17 = (f32[3,4]{1,0:T(4,128)S(1)}, f32[3,4]{1,0:T(4,128)}, u32[]{:S(2)}) copy-start(f32[3,4]{1,0:T(4,128)} %constant.134) | copy-start | bytes 148
  33.3 0.9 copy-start.15
  33.3 0.9 copy-start.16
  33.5 30.5 %copy-start.14 = (f32[64]{0:T(128)S(1)}, f32[64]{0:T(128)}, u32[]{:S(2)}) copy-start(f32[64]{0:T(128)} %constant.119.clone) | copy-start | bytes 772
  34.5 3.7 %collective-permute-start.1 = (bf16[2,64]{1,0:T(2,128)(2,1)S(1)}, bf16[2,64]{1,0:T(2,128)(2,1)S(1)}, u32[]{:S(2)}, u32[]{:S(2)}) collective-permute-start(bf16[2,64]{1,0:T(2,128)(2,1)S(1)} %broadcast_select_fusion.17), channel_id=1, source_target_pairs={{0,32},{32,0},{16,48},{48,16},{64,96},{96,64},{80,112},{112,80},{1... | collective-permute-start | bytes 776 | tf_op jit(solution)/shard_map/ppermute | solution.py:23
  38.1 5.6 %collective-permute-start.2 = (bf16[2,2,64]{2,1,0:T(2,128)(2,1)S(1)}, bf16[2,2,64]{2,1,0:T(2,128)(2,1)S(1)}, u32[]{:S(2)}, u32[]{:S(2)}) collective-permute-start(bf16[2,2,64]{2,1,0:T(2,128)(2,1)S(1)} %broadcast_select_fusion.15), channel_id=1, source_target_pairs={{0,64},{64,0},{16,80},{80,16},{32,96},{96,32},{48,112},{112,48},{1... | collective-permute-start | bytes 1544 | tf_op jit(solution)/shard_map/ppermute | solution.py:23
  43.7 3.7 %collective-permute-start.3 = (bf16[2,2,2,64]{3,2,1,0:T(2,128)(2,1)S(1)}, bf16[2,2,2,64]{3,2,1,0:T(2,128)(2,1)S(1)}, u32[]{:S(2)}, u32[]{:S(2)}) collective-permute-start(bf16[2,2,2,64]{3,2,1,0:T(2,128)(2,1)S(1)} %broadcast_select_fusion.11), channel_id=1, source_target_pairs={{0,1},{1,0},{2,3},{3,2},{4,5},{5,4},{6,7},{7,6},{8,9},{9,8},{10,11... | collective-permute-start | bytes 3080 | tf_op jit(solution)/shard_map/ppermute | solution.py:23
  47.4 5.4 %collective-permute-start.4 = (bf16[2,2,2,2,64]{4,3,2,1,0:T(2,128)(2,1)S(1)}, bf16[2,2,2,2,64]{4,3,2,1,0:T(2,128)(2,1)S(1)}, u32[]{:S(2)}, u32[]{:S(2)}) collective-permute-start(bf16[2,2,2,2,64]{4,3,2,1,0:T(2,128)(2,1)S(1)} %broadcast_select_fusion.8), channel_id=1, source_target_pairs={{0,2},{2,0},{1,3},{3,1},{4,6},{6,4},{5,7},{7,5},{8,10},{10,8},{9,1... | collective-permute-start | bytes 6152 | tf_op jit(solution)/shard_map/ppermute | solution.py:23
  52.8 3.7 %collective-permute-start.5 = (bf16[2,2,2,2,2,64]{5,4,3,2,1,0:T(2,128)(2,1)S(1)}, bf16[2,2,2,2,2,64]{5,4,3,2,1,0:T(2,128)(2,1)S(1)}, u32[]{:S(2)}, u32[]{:S(2)}) collective-permute-start(bf16[2,2,2,2,2,64]{5,4,3,2,1,0:T(2,128)(2,1)S(1)} %broadcast_select_fusion.5), channel_id=1, source_target_pairs={{0,4},{4,0},{1,5},{5,1},{2,6},{6,2},{3,7},{7,3},{8,12},{12,8},{9,1... | collective-permute-start | bytes 12296 | tf_op jit(solution)/shard_map/ppermute | solution.py:23
  56.6 5.3 %collective-permute-start.6 = (bf16[2,2,2,2,2,2,64]{6,5,4,3,2,1,0:T(2,128)(2,1)S(1)}, bf16[2,2,2,2,2,2,64]{6,5,4,3,2,1,0:T(2,128)(2,1)S(1)}, u32[]{:S(2)}, u32[]{:S(2)}) collective-permute-start(bf16[2,2,2,2,2,2,64]{6,5,4,3,2,1,0:T(2,128)(2,1)S(1)} %broadcast_select_fusion.2), channel_id=1, source_target_pairs={{0,8},{8,0},{1,9},{9,1},{2,10},{10,2},{3,11},{11,3},{4,12},{12,4},... | collective-permute-start | bytes 24584 | tf_op jit(solution)/shard_map/ppermute | solution.py:23
  64.8 29.7 %copy-start.4 = (f32[16,64,128]{2,1,0:T(8,128)S(1)}, f32[16,64,128]{2,1,0:T(8,128)}, u32[]{:S(2)}) copy-start(f32[16,64,128]{2,1,0:T(8,128)} %get-tuple-element.47) | copy-start | bytes 1572868
  94.4 1.2 copy-start.7
  95.5 2.2 %copy-start.9 = (bf16[128,128,1]{0,1,2:T(8,128)(2,1)S(1)}, bf16[128,128,1]{0,1,2:T(8,128)(2,1)}, u32[]{:S(2)}) copy-start(bf16[128,128,1]{0,1,2:T(8,128)(2,1)} %constant.250) | copy-start | bytes 98308
  97.6 1.3 %collective-permute-start.8 = (f32[2,2,2,2,2,2,192]{6,5,4,3,2,1,0:T(2,128)S(1)}, f32[2,2,2,2,2,2,192]{6,5,4,3,2,1,0:T(2,128)S(1)}, u32[]{:S(2)}, u32[]{:S(2)}) collective-permute-start(f32[2,2,2,2,2,2,192]{6,5,4,3,2,1,0:T(2,128)S(1)} %fusion.32), channel_id=1, source_target_pairs={{0,16},{16,0},{32,48},{48,32},{64,80},{80,64},{96,112},{112,96},{1... | collective-permute-start | bytes 147464 | tf_op jit(solution)/shard_map/ppermute | solution.py:23
  99.0 4.0 %collective-permute-start.9 = (f32[2,2,2,2,2,192]{5,4,3,2,1,0:T(2,128)S(1)}, f32[2,2,2,2,2,192]{5,4,3,2,1,0:T(2,128)S(1)}, u32[]{:S(2)}, u32[]{:S(2)}) collective-permute-start(f32[2,2,2,2,2,192]{5,4,3,2,1,0:T(2,128)S(1)} %fusion.36), channel_id=1, source_target_pairs={{0,32},{32,0},{16,48},{48,16},{64,96},{96,64},{80,112},{112,80},{1... | collective-permute-start | bytes 73736 | tf_op jit(solution)/shard_map/ppermute | solution.py:23
  101.8 17.4 %copy-start.6 = (bf16[64,64,64]{2,1,0:T(8,128)(2,1)S(1)}, bf16[64,64,64]{2,1,0:T(8,128)(2,1)}, u32[]{:S(2)}) copy-start(bf16[64,64,64]{2,1,0:T(8,128)(2,1)} %constant.248) | copy-start | bytes 1572868
  103.1 5.3 %collective-permute-start.10 = (f32[2,2,2,2,192]{4,3,2,1,0:T(2,128)S(1)}, f32[2,2,2,2,192]{4,3,2,1,0:T(2,128)S(1)}, u32[]{:S(2)}, u32[]{:S(2)}) collective-permute-start(f32[2,2,2,2,192]{4,3,2,1,0:T(2,128)S(1)} %select_bitcast_fusion), channel_id=1, source_target_pairs={{0,64},{64,0},{16,80},{80,16},{32,96},{96,32},{48,112},{112,48},{1... | collective-permute-start | bytes 36872 | tf_op jit(solution)/shard_map/ppermute | solution.py:23
  108.5 3.7 %collective-permute-start.11 = (f32[2,2,2,192]{3,2,1,0:T(2,128)S(1)}, f32[2,2,2,192]{3,2,1,0:T(2,128)S(1)}, u32[]{:S(2)}, u32[]{:S(2)}) collective-permute-start(f32[2,2,2,192]{3,2,1,0:T(2,128)S(1)} %bitcast.226), channel_id=1, source_target_pairs={{0,1},{1,0},{2,3},{3,2},{4,5},{5,4},{6,7},{7,6},{8,9},{9,8},{10,11... | collective-permute-start | bytes 18440 | tf_op jit(solution)/shard_map/ppermute | solution.py:23
  112.2 5.2 %collective-permute-start.12 = (f32[2,2,192]{2,1,0:T(2,128)S(1)}, f32[2,2,192]{2,1,0:T(2,128)S(1)}, u32[]{:S(2)}, u32[]{:S(2)}) collective-permute-start(f32[2,2,192]{2,1,0:T(2,128)S(1)} %bitcast.233), channel_id=1, source_target_pairs={{0,2},{2,0},{1,3},{3,1},{4,6},{6,4},{5,7},{7,5},{8,10},{10,8},{9,1... | collective-permute-start | bytes 9224 | tf_op jit(solution)/shard_map/ppermute | solution.py:23
  117.5 3.7 %collective-permute-start.13 = (f32[2,192]{1,0:T(2,128)S(1)}, f32[2,192]{1,0:T(2,128)S(1)}, u32[]{:S(2)}, u32[]{:S(2)}) collective-permute-start(f32[2,192]{1,0:T(2,128)S(1)} %bitcast.235), channel_id=1, source_target_pairs={{0,4},{4,0},{1,5},{5,1},{2,6},{6,2},{3,7},{7,3},{8,12},{12,8},{9,1... | collective-permute-start | bytes 4616 | tf_op jit(solution)/shard_map/ppermute | solution.py:23
  121.1 5.2 %collective-permute-start.14 = (f32[192]{0:T(256)S(1)}, f32[192]{0:T(256)S(1)}, u32[]{:S(2)}, u32[]{:S(2)}) collective-permute-start(f32[192]{0:T(256)S(1)} %bitcast.236), channel_id=1, source_target_pairs={{0,8},{8,0},{1,9},{9,1},{2,10},{10,2},{3,11},{11,3},{4,12},{12,4},... | collective-permute-start | bytes 2312 | tf_op jit(solution)/shard_map/ppermute | solution.py:23

commit v4 on v2

--- a/solution.py
+++ b/solution.py
@@ -220,12 +220,17 @@
     )
     target_point = jnp.transpose(
         target_point.reshape(3, drop_count, readers * point_count), (1, 2, 0)
-    ).reshape(-1)
+    )
+    target_square = jnp.sum(target_point * target_point, axis=2, keepdims=True) + SOFTENING
+    target_table = jnp.concatenate([target_point, target_square], axis=2).reshape(-1)
     source_radius = near_grid[:, 0].astype(jnp.float32)
     source_traction = near_grid[:, 1].astype(jnp.float32)
     cell_weight = jnp.broadcast_to(quad_weight[:, None], (nlat, nlon))
-    partial = near_field(target_point, source_radius, source_traction, normals, cell_weight)
-    contribution = jnp.sum(partial, axis=3) / (8.0 * math.pi)
+    partial = near_field(target_table, source_radius, source_traction, normals, cell_weight)
+    sums = jnp.sum(partial, axis=3)
+    contribution = (
+        sums[:, :3] + jnp.transpose(target_point, (0, 2, 1)) * sums[:, 3:]
+    ) / (8.0 * math.pi)
     contribution = jnp.transpose(
         contribution.reshape(drop_count, 3, readers, point_count), (0, 2, 1, 3)
     ).reshape(drop_count * readers, 3 * point_count)
@@ -263,38 +268,41 @@
     targets = o_ref.shape[2]
     chunks = r_ref.shape[1] // 8
     r = r_ref[0]
-    s_ref[0] = r * n_ref[0]
-    s_ref[1] = r * n_ref[1]
-    s_ref[2] = r * n_ref[2]
+    s_ref[0] = r
+    s_ref[1] = r * r
+    s_ref[2] = r + r
     s_ref[3] = q_ref[0] * r * r * w_ref[...]
 
     def body(t, carry):
-        base = (drop * targets + t) * 3
+        base = (drop * targets + t) * 4
         tx = t_ref[base]
         ty = t_ref[base + 1]
         tz = t_ref[base + 2]
-        ax = jnp.zeros((8, 128), jnp.float32)
-        ay = jnp.zeros((8, 128), jnp.float32)
-        az = jnp.zeros((8, 128), jnp.float32)
+        tt = t_ref[base + 3]
+        hx = jnp.zeros((8, 128), jnp.float32)
+        hy = jnp.zeros((8, 128), jnp.float32)
+        hz = jnp.zeros((8, 128), jnp.float32)
+        sq = jnp.zeros((8, 128), jnp.float32)
         for c in range(chunks):
             rows = pl.ds(c * 8, 8)
             nx = n_ref[0, rows, :]
             ny = n_ref[1, rows, :]
             nz = n_ref[2, rows, :]
-            dx = tx - s_ref[0, rows, :]
-            dy = ty - s_ref[1, rows, :]
-            dz = tz - s_ref[2, rows, :]
-            dd = dx * dx + dy * dy + dz * dz
-            inv = lax.rsqrt(dd + SOFTENING)
+            rr = s_ref[0, rows, :]
+            along = tx * nx + ty * ny + tz * nz
+            soft = (tt + s_ref[1, rows, :]) - s_ref[2, rows, :] * along
+            inv = lax.rsqrt(soft)
             w = s_ref[3, rows, :] * (inv * inv * inv)
-            dn = dx * nx + dy * ny + dz * nz
-            a = dd + 2.0 * SOFTENING
-            ax = ax + w * (nx * a + dx * dn)
-            ay = ay + w * (ny * a + dy * dn)
-            az = az + w * (nz * a + dz * dn)
-        o_ref[0, 0, pl.ds(t, 1), :] = jnp.sum(ax, axis=0, keepdims=True)
-        o_ref[0, 1, pl.ds(t, 1), :] = jnp.sum(ay, axis=0, keepdims=True)
-        o_ref[0, 2, pl.ds(t, 1), :] = jnp.sum(az, axis=0, keepdims=True)
+            dn = along - rr
+            h = w * ((soft + SOFTENING) - dn * rr)
+            hx = hx + h * nx
+            hy = hy + h * ny
+            hz = hz + h * nz
+            sq = sq + w * dn
+        o_ref[0, 0, pl.ds(t, 1), :] = jnp.sum(hx, axis=0, keepdims=True)
+        o_ref[0, 1, pl.ds(t, 1), :] = jnp.sum(hy, axis=0, keepdims=True)
+        o_ref[0, 2, pl.ds(t, 1), :] = jnp.sum(hz, axis=0, keepdims=True)
+        o_ref[0, 3, pl.ds(t, 1), :] = jnp.sum(sq, axis=0, keepdims=True)
         return carry
 
     lax.fori_loop(0, targets, body, 0)
@@ -302,7 +310,7 @@
 
 def near_field(target_point, source_radius, source_traction, normals, cell_weight):
     drops, nlat, nlon = source_radius.shape
-    targets = target_point.shape[0] // (3 * drops)
+    targets = target_point.shape[0] // (4 * drops)
     cells = drops * targets * nlat * nlon
     return pl.pallas_call(
         near_kernel,
@@ -314,11 +322,11 @@
             pl.BlockSpec((3, nlat, nlon), lambda s: (0, 0, 0)),
             pl.BlockSpec((nlat, nlon), lambda s: (0, 0)),
         ],
-        out_specs=pl.BlockSpec((1, 3, targets, nlon), lambda s: (s, 0, 0, 0)),
-        out_shape=jax.ShapeDtypeStruct((drops, 3, targets, nlon), jnp.float32),
+        out_specs=pl.BlockSpec((1, 4, targets, nlon), lambda s: (s, 0, 0, 0)),
+        out_shape=jax.ShapeDtypeStruct((drops, 4, targets, nlon), jnp.float32),
         scratch_shapes=[pltpu.VMEM((4, nlat, nlon), jnp.float32)],
         cost_estimate=pl.CostEstimate(
-            flops=36 * cells, transcendentals=cells, bytes_accessed=4 * drops * nlat * nlon * 2
+            flops=26 * cells, transcendentals=cells, bytes_accessed=4 * drops * nlat * nlon * 2
         ),
     )(target_point, source_radius, source_traction, normals, cell_weight)
 

time: 114 us -> 108 us (0.947)
  Pallas kernels: 29.6 us -> 22.8 us
    pallas_call x1, Pallas kernels: 29.6 us -> 22.8 us  [near_field(): pl.pallas_call(near_kernel, grid=(drops,), in_specs=[pl.BlockSpec(memory_...]
  transfers between devices with their start and end apart: 3 -> 3, of which waited for: 1 -> 1; matrix products, arithmetic and copies ran while one was open for 23% -> 25% of each run, Pallas kernels for 26% -> 21%
where the time goes in v4:
time: 108 us; the launch traced here: 106 us
  local copies, waits for them, and re-layouts  27.5 us (25%)
  Pallas kernels  22.8 us (21%)
  starting transfers between devices  21.5 us (20%)
  other arithmetic  14.2 us (13%)
  waiting for transfers between devices  9.57 us (9%)
  matrix products  9.4 us (9%)
  between operations  1.28 us (1%)
    pallas_call x1, Pallas kernels, near_field(): pl.pallas_call(near_kernel, grid=(drops,), in_specs=[pl.BlockSpec(memory_...  22.8 us
    all_to_all x1, starting transfers between devices, per_device(): lax.all_to_all(jnp.broadcast_to(own_points.reshape(1, -1), (devices, drop...  11.7 us
    all_to_all x1, starting transfers between devices, per_device(): lax.all_to_all(outgoing.reshape(devices, capacity, record.shape[1]), ('ro...  9.81 us
    all_to_all x1, waiting for transfers between devices, per_device(): lax.all_to_all(outgoing.reshape(devices, capacity, record.shape[1]), ('ro...  9.56 us
    another operation x2, local copies, waits for them, and re-layouts, legendre_synth(): parted = coeff.reshape(batch_size, degrees, 2, orders)  5.23 us
    transpose x1, local copies, waits for them, and re-layouts, legendre_synth(): return jnp.einsum('mjl,nlcm->njcm', legendre, parted, precision=SPECTRAL)  4.56 us
    dot_general x1, local copies, waits for them, and re-layouts, fourier_synth(): jnp.einsum('njw,wk->njk', partial_legendre.reshape(batch_size, nlat, two...  3.9 us
    mul x2, other arithmetic, prepare(): shape_part * (degree_value * (degree_value + 1.0) / (degrees * degrees))[...  3.18 us
  transfers between devices with their start and end apart: 3, of which 1 were waited for; matrix products, arithmetic and copies ran while one was open for 25% of the time, Pallas kernels for 21%

profile of v4, /device:TPU:0, one launch (start us, length us, event | category | flops | bytes accessed | tf_op | source)
XLA Modules:
  0.0 106.2 jit_solution(11915160941087203236)
XLA Ops:
  0.7 0.7 fusion.52
  1.5 1.7 %broadcast_multiply_fusion = (bf16[16,1,64,128]{3,2,1,0:T(8,128)(2,1)S(1)}, bf16[16,1,64,128]{3,2,1,0:T(8,128)(2,1)S(1)}, bf16[16,1,64,128]{3,2,1,0:T(8,128)(2,1)S(1)}, bf16[16,1,64,128]{3,2,1,0:T(8,128)(2,1)S(1)}) fusion(f32[64]{0:T(128)S(1)} %get-tuple-element.39, f32[16,64]{1,0:T(8,128)S(1)} %fusion.52, f32[64,128]{1,0:T(8,128)S(1)} %fusion.48, ...), kind=kLoop, calls=%fused_computation.46 | loop fusion | flops 1572864 | bytes 2658816 | tf_op jit(solution)/shard_map/mul | solution.py:112
  3.2 0.1 pad_maximum_fusion
  3.4 0.8 reshape_reshape.6
  4.2 4.4 %copy.87 = bf16[64,64,2,64]{1,0,2,3:T(8,128)(2,1)} copy(bf16[64,64,2,64]{3,2,1,0:T(2,128)(2,1)S(1)} %reshape_reshape.6) | data formatting | bytes 2097152 | tf_op jit(solution)/shard_map/reshape;reshape | solution.py:78
  8.6 2.3 %convolution_bitcast_fusion = bf16[64,64,2,64]{1,0,2,3:T(8,128)(2,1)S(1)} fusion(bf16[64,64,2,64]{1,0,2,3:T(8,128)(2,1)} %copy.87, bf16[64,64,64,1]{2,1,3,0:T(8,128)(2,1)S(1)} %copy-done.1), kind=kOutput, calls=%fused_computation | convolution fusion | flops 67108864 | bytes 2621440 | tf_op jit(solution)/shard_map/mjl,nlcm->njcm/dot_general | solution.py:79
  10.9 4.6 %copy.88 = bf16[64,64,2,64]{3,2,1,0:T(2,128)(2,1)} copy(bf16[64,64,2,64]{1,0,2,3:T(8,128)(2,1)S(1)} %convolution_bitcast_fusion) | data formatting | bytes 2097152 | tf_op jit(solution)/shard_map/mjl,nlcm->njcm/transpose | solution.py:79
  15.5 3.9 %dot_general.36 = bf16[16,4,64,128]{3,2,1,0:T(8,128)(2,1)S(1)} reshape(bf16[64,64,2,64]{3,2,1,0:T(2,128)(2,1)} %copy.88) | data formatting | bytes 2097152 | tf_op jit(solution)/shard_map/njw,wk->njk/dot_general | solution.py:84
  19.5 0.4 fusion
  19.9 1.2 %bitcast_convert_fusion.1 = (f32[16,64,128]{2,1,0:T(8,128)}, bf16[16,1,64,128]{3,2,0,1:T(8,128)(2,1)S(1)}, f32[16,64,128]{2,1,0:T(8,128)}, bf16[16,1,64,128]{3,2,0,1:T(8,128)(2,1)S(1)}) fusion(f32[16,4,64,128]{3,2,0,1:T(8,128)S(1)} %fusion, f32[16]{0:T(128)S(1)} %get-tuple-element.36, f32[16]{0:T(128)S(1)} %get-tuple-element.35), kind=kLoop, calls=%fused_computation.43 | loop fusion | flops 1310720 | bytes 3670144 | tf_op jit(solution)/shard_map/convert_element_type | solution.py:226
  21.1 0.8 pad_maximum_fusion.2
  21.9 1.1 slice.96
  23.0 0.1 broadcast_in_dim.6
  23.1 0.7 broadcast_in_dim.7
  23.8 11.7 %all-to-all-start = ((bf16[128,1,64]{2,1,0:T(2,128)(2,1)}), bf16[128,1,64]{2,1,0:T(2,128)(2,1)}, u32[]{:S(2)}, u32[]{:S(2)}) async-start(bf16[128,1,64]{2,1,0:T(2,128)(2,1)} %broadcast_in_dim.7), calls=%async_computation | async-start | bytes 131072 | tf_op jit(solution)/shard_map/all_to_all | solution.py:204
  35.5 0.7 fusion.46
  36.2 0.7 fusion.47
  36.8 1.7 %fusion.65 = (f32[4,1,64,64]{3,2,1,0:T(8,128)}, f32[4,1,64,64]{3,2,1,0:T(8,128)S(1)}, f32[4,1,64,64]{3,2,1,0:T(8,128)S(1)}) fusion(f32[4,3,64,64]{3,2,1,0:T(8,128)} %param.15), kind=kLoop, calls=%fused_computation.116 | loop fusion | bytes 393216 | tf_op jit(solution)/shard_map/slice | solution.py:110
  38.6 0.1 copy.128
  38.7 0.1 copy.129
  38.8 1.0 copy.127
  39.8 1.4 %broadcast_multiply_fusion.2 = (bf16[4,1,64,64]{2,3,1,0:T(8,128)(2,1)}, bf16[4,1,64,64]{2,3,1,0:T(8,128)(2,1)}) fusion(f32[64]{0:T(128)} %copy-done.17, f32[4,1,64,64]{2,3,1,0:T(8,128)S(1)} %copy.127, f32[64,64]{0,1:T(8,128)} %fusion.47), kind=kLoop, calls=%fused_computation.73 | loop fusion | flops 65536 | bytes 147712 | tf_op jit(solution)/shard_map/mul | solution.py:112
  41.2 0.8 broadcast_multiply_fusion.1
  42.0 0.9 pad_maximum_fusion.1
  43.0 0.4 convolution_bitcast_fusion.3
  43.4 2.0 %fusion.66 = (bf16[16,64,128]{2,1,0:T(8,128)(2,1)}, f32[16,64,128]{2,1,0:T(8,128)}) fusion(bf16[2,64,128]{2,1,0:T(8,128)(2,1)} %constant.201, s32[]{:T(128)S(6)} %select_n.46, bf16[16,64,2,32]{1,0,2,3:T(8,128)(2,1)S(1)} %convolution_bitcast_fusion.3), kind=kOutput, calls=%fused_computation.117 | convolution fusion | flops 16908288 | bytes 933892 | tf_op jit(solution)/shard_map/njw,wk->njk/dot_general | solution.py:84
  45.5 0.6 multiply_add_fusion
  46.1 0.1 fusion.39
  46.2 0.2 reduce_window_sum.11
  46.4 0.2 select_reduce_fusion
  46.6 1.8 %convolution_multiply_fusion = bf16[16,64,128]{2,1,0:T(8,128)(2,1)} fusion(bf16[128,128,1]{1,0,2:T(8,128)(2,1)} %constant.197, f32[16,4,64,128]{3,2,0,1:T(8,128)S(1)} %fusion, f32[64]{0:T(128)} %constant.112.clone, f32[16]{0:T(128)} %copy-done.19, f32[16]{0:T(128)} %copy-done.18), kind=kOutput, calls=%fused_computation.7 | convolution fusion | flops 34603008 | bytes 1868160 | tf_op jit(solution)/shard_map/bjk,wk->bjw/dot_general | solution.py:95
  48.4 1.2 %reshape.237 = bf16[16,64,2,64]{3,2,1,0:T(2,128)(2,1)S(1)} reshape(bf16[16,64,128]{2,1,0:T(8,128)(2,1)} %convolution_multiply_fusion) | data formatting | bytes 524288 | tf_op jit(solution)/shard_map/reshape | solution.py:98
  49.6 0.7 copy.92
  50.3 0.4 convolution_bitcast_fusion.1
  50.7 0.7 copy.93
  51.4 0.6 reshape.238
  52.0 1.0 multiply_multiply_fusion.5
  53.3 0.1 add.148
  53.4 0.1 add.149
  53.6 0.1 add.150
  53.7 0.1 mul.389
  54.0 1.0 reduce
  55.0 0.6 reshape.244
  55.7 0.4 fusion.6
  56.2 0.2 copy.111
  56.4 0.8 reshape.245.t_ref
  57.1 0.7 broadcast_in_dim.8.w_ref
  57.8 22.8 %shard_map.139 = f32[16,4,32,128]{3,2,1,0:T(8,128)} custom-call(f32[2048]{0:T(1024)} %reshape.245.t_ref, f32[16,64,128]{2,1,0:T(8,128)} %get-tuple-element.14.r_ref, f32[16,64,128]{2,1,0:T(8,128)} %get-tuple-element.22.q_ref, f32[3,64,128]{2,1,0:T(8,128)} %constant.113.clone.n_ref, f32[64,128]{1,0:T(8,128)} %broadcast_in_dim.8.w_ref), custom_call_target="tpu_custom_call" | custom-call | flops 109051904 | bytes 1048576 | tf_op jit(solution)/shard_map/pallas_call | solution.py:315
  80.7 1.7 %reduce_sum.29 = f32[16,4,32]{2,1,0:T(4,128)S(1)} reduce(f32[16,4,32,128]{3,2,1,0:T(8,128)} %shard_map.139, f32[]{:T(128)} %constant.107.clone.1), dimensions={3}, to_apply=%region_3.4 | reduce | flops 260096 | bytes 1056772 | tf_op jit(solution)/shard_map/reduce_sum | solution.py:230
  82.5 0.1 copy.113
  82.6 0.1 reshape.247
  82.7 1.0 fusion.35
  83.7 9.8 %all-to-all-start.1 = ((f32[128,2,13]{2,1,0:T(2,128)}), f32[128,2,13]{2,1,0:T(2,128)S(1)}, u32[]{:S(2)}, u32[]{:S(2)}) async-start(f32[128,2,13]{2,1,0:T(2,128)} %bitcast.34), calls=%async_computation.1 | async-start | bytes 262144 | tf_op jit(solution)/shard_map/all_to_all | solution.py:251
  93.5 9.6 %all-to-all-done.1 = f32[128,2,13]{2,1,0:T(2,128)S(1)} async-done(((f32[128,2,13]{2,1,0:T(2,128)}), f32[128,2,13]{2,1,0:T(2,128)S(1)}, u32[]{:S(2)}, u32[]{:S(2)}) %all-to-all-start.1) | async-done | bytes 13344 | tf_op jit(solution)/shard_map/all_to_all | solution.py:251
  103.1 0.2 slice_reduce_fusion
  103.3 0.3 fusion.28
  103.6 0.1 copy.117
  103.7 0.7 reshape.251
  104.5 0.2 convolution_multiply_fusion.1
  104.7 0.1 reshape.241
  104.8 0.2 constant_dynamic-slice_fusion
  105.0 0.1 copy.133
  105.2 0.3 convolution_bitcast_fusion.4
  105.5 0.8 copy.118
  (76 shorter events, 1.2 us)
Async XLA Ops:
  0.6 52.4 %copy-start = (f32[256,2]{0,1:T(2,128)S(1)}, f32[256,2]{0,1:T(2,128)}, u32[]{:S(2)}) copy-start(f32[256,2]{0,1:T(2,128)} %param.16) | copy-start | bytes 6148
  0.7 2.5 %copy-start.16 = (f32[64]{0:T(128)}, f32[64]{0:T(128)S(1)}, u32[]{:S(2)}) copy-start(f32[64]{0:T(128)S(1)} %get-tuple-element.40) | copy-start | bytes 772
  0.7 2.5 %copy-start.17 = (f32[64]{0:T(128)}, f32[64]{0:T(128)S(1)}, u32[]{:S(2)}) copy-start(f32[64]{0:T(128)S(1)} %get-tuple-element.39) | copy-start | bytes 772
  0.7 2.5 %copy-start.6 = (f32[64,128]{1,0:T(8,128)}, f32[64,128]{1,0:T(8,128)S(1)}, u32[]{:S(2)}) copy-start(f32[64,128]{1,0:T(8,128)S(1)} %fusion.48) | copy-start | bytes 98308
  4.2 4.4 %copy-start.1 = (bf16[64,64,64,1]{2,1,3,0:T(8,128)(2,1)S(1)}, bf16[64,64,64,1]{2,1,3,0:T(8,128)(2,1)}, u32[]{:S(2)}) copy-start(bf16[64,64,64,1]{2,1,3,0:T(8,128)(2,1)} %constant.199) | copy-start | bytes 1572868
  15.5 3.9 %copy-start.20 = (f32[16,2]{0,1:T(2,128)S(1)}, f32[16,2]{0,1:T(2,128)}, u32[]{:S(2)}) copy-start(f32[16,2]{0,1:T(2,128)} %param.14) | copy-start | bytes 388
  15.5 3.9 %copy-start.9 = (bf16[128,128,1,1]{1,0,2,3:T(8,128)(2,1)S(1)}, bf16[128,128,1,1]{1,0,2,3:T(8,128)(2,1)}, u32[]{:S(2)}) copy-start(bf16[128,128,1,1]{1,0,2,3:T(8,128)(2,1)} %constant.198) | copy-start | bytes 98308
  19.4 1.7 %copy-start.18 = (f32[16]{0:T(128)}, f32[16]{0:T(128)S(1)}, u32[]{:S(2)}) copy-start(f32[16]{0:T(128)S(1)} %get-tuple-element.35) | copy-start | bytes 196
  19.4 1.6 %copy-start.19 = (f32[16]{0:T(128)}, f32[16]{0:T(128)S(1)}, u32[]{:S(2)}) copy-start(f32[16]{0:T(128)S(1)} %get-tuple-element.36) | copy-start | bytes 196
  21.1 21.9 %copy-start.4 = (bf16[64,64,64]{2,1,0:T(8,128)(2,1)S(1)}, bf16[64,64,64]{2,1,0:T(8,128)(2,1)}, u32[]{:S(2)}) copy-start(bf16[64,64,64]{2,1,0:T(8,128)(2,1)} %constant.200) | copy-start | bytes 1572868
  23.8 30.2 %all-to-all-start = ((bf16[128,1,64]{2,1,0:T(2,128)(2,1)}), bf16[128,1,64]{2,1,0:T(2,128)(2,1)}, u32[]{:S(2)}, u32[]{:S(2)}) async-start(bf16[128,1,64]{2,1,0:T(2,128)(2,1)} %broadcast_in_dim.7), calls=%async_computation | async-start | bytes 131072 | tf_op jit(solution)/shard_map/all_to_all | solution.py:204
  38.6 6.8 %copy-start.10 = (s32[16,8]{0,1:T(8,128)S(1)}, s32[16,8]{0,1:T(8,128)}, u32[]{:S(2)}) copy-start(s32[16,8]{0,1:T(8,128)} %param.18) | copy-start | bytes 1540
  42.0 3.4 %copy-start.14 = (s32[16,8]{0,1:T(8,128)S(1)}, s32[16,8]{0,1:T(8,128)}, u32[]{:S(2)}) copy-start(s32[16,8]{0,1:T(8,128)} %param.19) | copy-start | bytes 1540
  43.4 6.9 %copy-start.2 = (bf16[64,64,64,1]{2,1,3,0:T(8,128)(2,1)S(1)}, bf16[64,64,64,1]{2,1,3,0:T(8,128)(2,1)}, u32[]{:S(2)}) copy-start(bf16[64,64,64,1]{2,1,3,0:T(8,128)(2,1)} %constant.199) | copy-start | bytes 1572868
  45.4 59.0 %collective-permute-start = (bf16[16,64,128]{2,1,0:T(8,128)(2,1)}, bf16[16,64,128]{2,1,0:T(8,128)(2,1)S(1)}, u32[]{:S(2)}, u32[]{:S(2)}) collective-permute-start(bf16[16,64,128]{2,1,0:T(8,128)(2,1)} %get-tuple-element.37), channel_id=1, source_target_pairs={{0,16},{16,0},{32,48},{48,32},{64,80},{80,64},{96,112},{112,96},{1... | collective-permute-start | bytes 786440 | tf_op jit(solution)/shard_map/ppermute | solution.py:23
  50.7 1.3 %copy-start.7 = (f32[64,128]{1,0:T(8,128)S(1)}, f32[64,128]{1,0:T(8,128)}, u32[]{:S(2)}) copy-start(f32[64,128]{1,0:T(8,128)} %copy-done.6) | copy-start | bytes 98308
  50.7 2.4 %copy-start.12 = (s32[16,8]{0,1:T(8,128)S(1)}, s32[16,8]{0,1:T(8,128)}, u32[]{:S(2)}) copy-start(s32[16,8]{0,1:T(8,128)} %get-tuple-element.31) | copy-start | bytes 1540
  50.7 2.6 %copy-start.13 = (f32[3,16,8]{1,2,0:T(8,128)S(1)}, f32[3,16,8]{1,2,0:T(8,128)}, u32[]{:S(2)}) copy-start(f32[3,16,8]{1,2,0:T(8,128)} %param.17) | copy-start | bytes 4612
  51.4 2.3 %copy-start.15 = (f32[3,4]{1,0:T(4,128)S(1)}, f32[3,4]{1,0:T(4,128)}, u32[]{:S(2)}) copy-start(f32[3,4]{1,0:T(4,128)} %constant.123) | copy-start | bytes 148
  51.4 2.4 %copy-start.11 = (f32[16,8]{0,1:T(8,128)S(1)}, f32[16,8]{0,1:T(8,128)}, u32[]{:S(2)}) copy-start(f32[16,8]{0,1:T(8,128)} %get-tuple-element.32) | copy-start | bytes 1540
  52.0 5.1 %copy-start.21 = (f32[64]{0:T(128)S(1)}, f32[64]{0:T(128)}, u32[]{:S(2)}) copy-start(f32[64]{0:T(128)} %constant.112.clone) | copy-start | bytes 772
  80.6 23.8 %copy-start.3 = (f32[16,64,128]{2,1,0:T(8,128)S(1)}, f32[16,64,128]{2,1,0:T(8,128)}, u32[]{:S(2)}) copy-start(f32[16,64,128]{2,1,0:T(8,128)} %get-tuple-element.38) | copy-start | bytes 1572868
  80.6 23.8 %copy-start.22 = (bf16[128,128,1]{1,0,2:T(8,128)(2,1)S(1)}, bf16[128,128,1]{1,0,2:T(8,128)(2,1)}, u32[]{:S(2)}) copy-start(bf16[128,128,1]{1,0,2:T(8,128)(2,1)} %constant.197) | copy-start | bytes 98308
  80.6 24.5 %copy-start.5 = (bf16[64,64,64]{2,1,0:T(8,128)(2,1)S(1)}, bf16[64,64,64]{2,1,0:T(8,128)(2,1)}, u32[]{:S(2)}) copy-start(bf16[64,64,64]{2,1,0:T(8,128)(2,1)} %constant.200) | copy-start | bytes 1572868
  82.6 22.8 %copy-start.8 = (f32[64,64]{0,1:T(8,128)S(1)}, f32[64,64]{0,1:T(8,128)}, u32[]{:S(2)}) copy-start(f32[64,64]{0,1:T(8,128)} %fusion.47) | copy-start | bytes 49156
  83.7 19.4 %all-to-all-start.1 = ((f32[128,2,13]{2,1,0:T(2,128)}), f32[128,2,13]{2,1,0:T(2,128)S(1)}, u32[]{:S(2)}, u32[]{:S(2)}) async-start(f32[128,2,13]{2,1,0:T(2,128)} %bitcast.34), calls=%async_computation.1 | async-start | bytes 262144 | tf_op jit(solution)/shard_map/all_to_all | solution.py:251

commit v5 on v4

--- a/solution.py
+++ b/solution.py
@@ -73,7 +73,7 @@
 
 
 def legendre_synth(coeff, legendre):
-    batch_size, degrees, coef_width = coeff.shape
+    batch_size, degrees, _ = coeff.shape
     orders = legendre.shape[0]
     parted = coeff.reshape(batch_size, degrees, 2, orders)
     return jnp.einsum("mjl,nlcm->njcm", legendre, parted, precision=SPECTRAL)
@@ -90,7 +90,7 @@
 
 
 def analysis_fourier(traction_grid, fourier, quad_weight):
-    batch_size, nlat, nlon = traction_grid.shape
+    batch_size, nlat, _ = traction_grid.shape
     projected = (
         jnp.einsum("bjk,wk->bjw", traction_grid, fourier, precision=SPECTRAL)
         * quad_weight[None, :, None]
@@ -126,28 +126,10 @@
     return (radius, traction_grid)
 
 
-def velocity_terms(
-    radius, traction_grid, spacing, target_radius, cell_weight, cell_normal, target_normal
-):
-    load_grid = traction_grid * radius * radius * cell_weight[None, :]
-    target_point = spacing[:, :, None] + target_radius[None] * target_normal[:, None, :]
-    surface_point = radius[None] * cell_normal[:, None, :]
-    offset = target_point[:, :, :, None] - surface_point[:, :, None, :]
-    distance_sq = jnp.sum(offset * offset, axis=0)
-    softened = distance_sq + SOFTENING
-    weight = load_grid[:, None, :] / (softened * jnp.sqrt(softened))
-    normal_dot = jnp.sum(offset * cell_normal[:, None, None, :], axis=0)
-    stokeslet = weight[None] * (
-        cell_normal[:, None, None, :] * (distance_sq + 2.0 * SOFTENING)[None]
-        + offset * normal_dot[None]
-    )
-    return jnp.sum(stokeslet, axis=3) / (8.0 * math.pi)
-
-
 def per_device(
     coeffs, degree, material, split_coeffs, split_material, separation, reader_dev, reader_slot
 ):
-    drop_count, fields, degrees, coef_width = coeffs.shape
+    drop_count, _, degrees, coef_width = coeffs.shape
     legendre, fourier, quad_weight, normals = spectral_tables(degrees)
     nlat = legendre.shape[1]
     nlon = fourier.shape[1]
@@ -163,10 +145,6 @@
     )
     surface = fourier_synth(partial_legendre, fourier).reshape(drop_count, 4, nlat, nlon)
     radius, traction_grid = traction(surface, material)
-    traction_coeffs = (
-        analysis_legendre(analysis_fourier(traction_grid, fourier, quad_weight), legendre)
-        * keep_mask
-    )
     split_count = split_coeffs.shape[0]
     half_width = split_coeffs.shape[3]
     half_orders = half_width // 2
@@ -189,12 +167,7 @@
     split_surface = partial_surface + from_partner(
         partial_surface.astype(jnp.bfloat16), "row", 0
     ).astype(partial_surface.dtype)
-    split_radius, split_grid = traction(
-        split_surface.reshape(split_count, 4, nlat, nlon), own_material
-    )
-    coef_grid = analysis_fourier(split_grid, fourier, quad_weight)
-    own_grid = lax.dynamic_slice_in_dim(coef_grid, half_index * half_orders, half_orders, 3)
-    split_traction = analysis_legendre(own_grid, own_legendre) * keep_half[None]
+    _, split_grid = traction(split_surface.reshape(split_count, 4, nlat, nlon), own_material)
     near_grid = jnp.stack([radius, traction_grid], axis=1).astype(jnp.bfloat16)
     point_grid = near_grid[:, 0, nlat // 4 :: nlat // 2, :: nlon // 2]
     point_count = point_grid.shape[1] * point_grid.shape[2]
@@ -227,6 +200,9 @@
     source_traction = near_grid[:, 1].astype(jnp.float32)
     cell_weight = jnp.broadcast_to(quad_weight[:, None], (nlat, nlon))
     partial = near_field(target_table, source_radius, source_traction, normals, cell_weight)
+    partial, traction_grid, split_grid = lax.optimization_barrier(
+        (partial, traction_grid, split_grid)
+    )
     sums = jnp.sum(partial, axis=3)
     contribution = (
         sums[:, :3] + jnp.transpose(target_point, (0, 2, 1)) * sums[:, 3:]
@@ -260,6 +236,13 @@
     ).astype(jnp.float32)
     mine = jnp.dot(jnp.transpose(slot_pick), incoming[:, :-1], precision=HIGH)
     near_velocity = jnp.transpose(mine.reshape(drop_count, 3, point_count), (1, 0, 2))
+    traction_coeffs = (
+        analysis_legendre(analysis_fourier(traction_grid, fourier, quad_weight), legendre)
+        * keep_mask
+    )
+    coef_grid = analysis_fourier(split_grid, fourier, quad_weight)
+    own_grid = lax.dynamic_slice_in_dim(coef_grid, half_index * half_orders, half_orders, 3)
+    split_traction = analysis_legendre(own_grid, own_legendre) * keep_half[None]
     return (traction_coeffs, split_traction, near_velocity.reshape(3, drop_count * point_count))
 
 

time: 108 us -> 100 us (0.926)
  matrix products: 9.4 us -> 6.09 us
  other arithmetic: 14.2 us -> 11.7 us
    dot_general x2, matrix products: 2.4 us -> 0.7 us  [fourier_synth(): jnp.einsum('njw,wk->njk', partial_legendre.reshape(batch_size, nlat, two...]
    dot_general x2, matrix products: 2 us -> 0.4 us  [analysis_fourier(): jnp.einsum('bjk,wk->bjw', traction_grid, fourier, precision=SPECTRAL)]
    reduce_sum x1, other arithmetic: 1.69 us -> 0.37 us  [per_device(): sums = jnp.sum(partial, axis=3)]
    unnamed x53 -> x49, local copies, waits for them, and re-layouts: 2.34 us -> 2.33 us
  transfers between devices with their start and end apart: 3 -> 3, of which waited for: 1 -> 1; matrix products, arithmetic and copies ran while one was open for 25% -> 14% of each run, Pallas kernels for 21% -> 23%
where the time goes in v5:
time: 100 us; the launch traced here: 99 us
  local copies, waits for them, and re-layouts  26.6 us (27%)
  Pallas kernels  22.8 us (23%)
  starting transfers between devices  21.7 us (22%)
  other arithmetic  11.7 us (12%)
  waiting for transfers between devices  8.79 us (9%)
  matrix products  6.09 us (6%)
  between operations  1.3 us (1%)
    pallas_call x1, Pallas kernels, near_field(): pl.pallas_call(near_kernel, grid=(drops,), in_specs=[pl.BlockSpec(memory_...  22.8 us
    all_to_all x1, starting transfers between devices, per_device(): lax.all_to_all(jnp.broadcast_to(own_points.reshape(1, -1), (devices, drop...  11.7 us
    all_to_all x1, starting transfers between devices, per_device(): lax.all_to_all(outgoing.reshape(devices, capacity, record.shape[1]), ('ro...  9.79 us
    all_to_all x1, waiting for transfers between devices, per_device(): lax.all_to_all(outgoing.reshape(devices, capacity, record.shape[1]), ('ro...  8.78 us
    another operation x2, local copies, waits for them, and re-layouts, legendre_synth(): parted = coeff.reshape(batch_size, degrees, 2, orders)  5.25 us
    transpose x1, local copies, waits for them, and re-layouts, legendre_synth(): return jnp.einsum('mjl,nlcm->njcm', legendre, parted, precision=SPECTRAL)  4.57 us
    dot_general x1, local copies, waits for them, and re-layouts, fourier_synth(): jnp.einsum('njw,wk->njk', partial_legendre.reshape(batch_size, nlat, two...  3.9 us
    dot_general x2, matrix products, legendre_synth(): return jnp.einsum('mjl,nlcm->njcm', legendre, parted, precision=SPECTRAL)  2.69 us
  transfers between devices with their start and end apart: 3, of which 1 were waited for; matrix products, arithmetic and copies ran while one was open for 14% of the time, Pallas kernels for 23%

profile of v5, /device:TPU:0, one launch (start us, length us, event | category | flops | bytes accessed | tf_op | source)
XLA Modules:
  0.0 99.0 jit_solution(5473337902233210681)
XLA Ops:
  0.7 0.7 fusion.38
  1.4 1.7 %broadcast_multiply_fusion = (bf16[16,1,64,128]{3,2,1,0:T(8,128)(2,1)S(1)}, bf16[16,1,64,128]{3,2,1,0:T(8,128)(2,1)S(1)}, bf16[16,1,64,128]{3,2,1,0:T(8,128)(2,1)S(1)}, bf16[16,1,64,128]{3,2,1,0:T(8,128)(2,1)S(1)}) fusion(f32[64]{0:T(128)S(1)} %get-tuple-element.45, f32[16,64]{1,0:T(8,128)S(1)} %fusion.38, f32[64,128]{1,0:T(8,128)S(1)} %fusion.34, ...), kind=kLoop, calls=%fused_computation.40 | loop fusion | flops 1572864 | bytes 2658816 | tf_op jit(solution)/shard_map/mul | solution.py:112
  3.2 0.1 pad_maximum_fusion
  3.4 0.9 reshape_reshape.6
  4.2 4.4 %copy.89 = bf16[64,64,2,64]{1,0,2,3:T(8,128)(2,1)} copy(bf16[64,64,2,64]{3,2,1,0:T(2,128)(2,1)S(1)} %reshape_reshape.6) | data formatting | bytes 2097152 | tf_op jit(solution)/shard_map/reshape;reshape | solution.py:78
  8.6 2.3 %convolution_bitcast_fusion = bf16[64,64,2,64]{1,0,2,3:T(8,128)(2,1)S(1)} fusion(bf16[64,64,2,64]{1,0,2,3:T(8,128)(2,1)} %copy.89, bf16[64,64,64,1]{2,1,3,0:T(8,128)(2,1)S(1)} %copy-done.1), kind=kOutput, calls=%fused_computation | convolution fusion | flops 67108864 | bytes 2621440 | tf_op jit(solution)/shard_map/mjl,nlcm->njcm/dot_general | solution.py:79
  10.9 4.6 %copy.90 = bf16[64,64,2,64]{3,2,1,0:T(2,128)(2,1)} copy(bf16[64,64,2,64]{1,0,2,3:T(8,128)(2,1)S(1)} %convolution_bitcast_fusion) | data formatting | bytes 2097152 | tf_op jit(solution)/shard_map/mjl,nlcm->njcm/transpose | solution.py:79
  15.5 3.9 %dot_general.36 = bf16[16,4,64,128]{3,2,1,0:T(8,128)(2,1)S(1)} reshape(bf16[64,64,2,64]{3,2,1,0:T(2,128)(2,1)} %copy.90) | data formatting | bytes 2097152 | tf_op jit(solution)/shard_map/njw,wk->njk/dot_general | solution.py:84
  19.5 0.4 fusion
  19.9 1.2 %bitcast_convert_fusion.1 = (f32[16,64,128]{2,1,0:T(8,128)}, bf16[16,1,64,128]{3,2,0,1:T(8,128)(2,1)S(1)}, f32[16,64,128]{2,1,0:T(8,128)}, bf16[16,1,64,128]{3,2,0,1:T(8,128)(2,1)S(1)}) fusion(f32[16,4,64,128]{3,2,0,1:T(8,128)S(1)} %fusion, f32[16]{0:T(128)S(1)} %get-tuple-element.42, f32[16]{0:T(128)S(1)} %get-tuple-element.41), kind=kLoop, calls=%fused_computation.39 | loop fusion | flops 1310720 | bytes 3670144 | tf_op jit(solution)/shard_map/convert_element_type | solution.py:199
  21.1 0.8 pad_maximum_fusion.1
  21.9 1.1 %slice.88 = bf16[16,1,2,2]{3,2,0,1:T(2,128)(2,1)S(1)} slice(bf16[16,2,64,128]{3,2,0,1:T(8,128)(2,1)} %pad_maximum_fusion.1), slice={[0:16:1], [0:1:1], [16:64:32], [0:128:64]} | slice | bytes 256 | tf_op jit(solution)/shard_map/slice | solution.py:172
  23.0 0.1 broadcast_in_dim.6
  23.1 0.7 broadcast_in_dim.7
  23.8 11.7 %all-to-all-start = ((bf16[128,1,64]{2,1,0:T(2,128)(2,1)}), bf16[128,1,64]{2,1,0:T(2,128)(2,1)}, u32[]{:S(2)}, u32[]{:S(2)}) async-start(bf16[128,1,64]{2,1,0:T(2,128)(2,1)} %broadcast_in_dim.7), calls=%async_computation | async-start | bytes 131072 | tf_op jit(solution)/shard_map/all_to_all | solution.py:177
  35.5 0.7 fusion.32
  36.2 0.7 fusion.33
  36.8 1.7 %fusion.49 = (f32[4,1,64,64]{3,2,1,0:T(8,128)}, f32[4,1,64,64]{3,2,1,0:T(8,128)S(1)}, f32[4,1,64,64]{3,2,1,0:T(8,128)S(1)}) fusion(f32[4,3,64,64]{3,2,1,0:T(8,128)} %param.15), kind=kLoop, calls=%fused_computation.104 | loop fusion | bytes 393216 | tf_op jit(solution)/shard_map/slice | solution.py:110
  38.6 0.1 copy.128
  38.7 0.1 copy.129
  38.8 1.0 %copy.127 = f32[4,1,64,64]{2,3,1,0:T(8,128)S(1)} copy(f32[4,1,64,64]{3,2,1,0:T(8,128)} %get-tuple-element.32) | data formatting | bytes 131072
  39.8 0.8 broadcast_multiply_fusion.2
  40.6 0.8 broadcast_multiply_fusion.1
  41.5 0.4 convolution_bitcast_fusion.3
  41.9 0.3 fusion.51
  42.2 0.3 collective-permute-start
  42.5 0.9 fusion.11
  43.7 0.2 reduce_window_sum.11
  43.9 0.2 select_reduce_fusion
  44.1 0.1 mul.345
  44.5 0.1 add.132
  44.6 0.1 add.133
  44.7 0.1 add.134
  45.0 1.0 %reduce = bf16[128,64]{1,0:T(8,128)(2,1)S(1)} reduce(bf16[128,1,64]{2,1,0:T(2,128)(2,1)} %all-to-all-done, bf16[]{:T(256)} %constant.127), dimensions={1}, to_apply=%all_to_all.7.reduce_sub_computation | reduce | bytes 32770 | tf_op jit(solution)/shard_map/all_to_all | solution.py:177
  46.0 0.6 reshape.237
  46.6 0.4 fusion.6
  47.2 0.2 copy.98
  47.4 0.8 reshape.238.t_ref
  48.1 0.7 broadcast_in_dim.8.w_ref
  48.8 22.8 %shard_map.139 = f32[16,4,32,128]{3,2,1,0:T(8,128)} custom-call(f32[2048]{0:T(1024)} %reshape.238.t_ref, f32[16,64,128]{2,1,0:T(8,128)} %get-tuple-element.22.r_ref, f32[16,64,128]{2,1,0:T(8,128)} %get-tuple-element.28.q_ref, f32[3,64,128]{2,1,0:T(8,128)} %constant.113.clone.n_ref, f32[64,128]{1,0:T(8,128)} %broadcast_in_dim.8.w_ref), custom_call_target="tpu_custom_call" | custom-call | flops 109051904 | bytes 1048576 | tf_op jit(solution)/shard_map/pallas_call | solution.py:298
  71.7 0.1 fusion.18
  71.8 0.2 convolution_multiply_fusion
  72.0 0.2 reshape.241
  72.3 0.7 copy.107
  73.0 0.4 convolution_bitcast_fusion.1
  73.4 0.7 copy.108
  74.1 0.6 reshape.242
  74.7 1.0 %multiply_multiply_fusion.5 = f32[16,64,128]{2,1,0:T(8,128)} fusion(f32[16,64,128]{2,1,0:T(8,128)S(1)} %reshape.242, f32[16,64]{1,0:T(8,128)S(1)} %fusion.38, f32[64,128]{1,0:T(8,128)S(1)} %copy-done.7), kind=kLoop, calls=%fused_computation.35 | loop fusion | flops 262144 | bytes 1085440 | tf_op jit(solution)/shard_map/mul | solution.py:240
  75.7 0.2 convolution_multiply_fusion.1
  75.9 0.1 reshape.243
  76.0 0.2 constant_dynamic-slice_fusion
  76.2 0.1 copy.133
  76.3 0.3 convolution_bitcast_fusion.4
  76.6 0.4 reduce_sum.29
  77.2 0.1 copy.113
  77.3 0.1 reshape.247
  77.4 1.0 fusion.24
  78.4 9.8 %all-to-all-start.1 = ((f32[128,2,13]{2,1,0:T(2,128)}), f32[128,2,13]{2,1,0:T(2,128)S(1)}, u32[]{:S(2)}, u32[]{:S(2)}) async-start(f32[128,2,13]{2,1,0:T(2,128)} %bitcast.35), calls=%async_computation.1 | async-start | bytes 262144 | tf_op jit(solution)/shard_map/all_to_all | solution.py:227
  88.2 0.8 copy.118
  88.9 8.8 %all-to-all-done.1 = f32[128,2,13]{2,1,0:T(2,128)S(1)} async-done(((f32[128,2,13]{2,1,0:T(2,128)}), f32[128,2,13]{2,1,0:T(2,128)S(1)}, u32[]{:S(2)}, u32[]{:S(2)}) %all-to-all-start.1) | async-done | bytes 13344 | tf_op jit(solution)/shard_map/all_to_all | solution.py:227
  97.7 0.2 slice_reduce_fusion
  97.9 0.3 fusion.19
  98.2 0.1 copy.117
  98.3 0.7 reshape.251
  (74 shorter events, 1.4 us)
Async XLA Ops:
  0.6 42.8 %copy-start = (f32[256,2]{0,1:T(2,128)S(1)}, f32[256,2]{0,1:T(2,128)}, u32[]{:S(2)}) copy-start(f32[256,2]{0,1:T(2,128)} %param.16) | copy-start | bytes 6148
  0.7 2.5 %copy-start.18 = (f32[64]{0:T(128)}, f32[64]{0:T(128)S(1)}, u32[]{:S(2)}) copy-start(f32[64]{0:T(128)S(1)} %get-tuple-element.46) | copy-start | bytes 772
  0.7 2.5 %copy-start.19 = (f32[64]{0:T(128)}, f32[64]{0:T(128)S(1)}, u32[]{:S(2)}) copy-start(f32[64]{0:T(128)S(1)} %get-tuple-element.45) | copy-start | bytes 772
  1.4 1.8 %copy-start.6 = (f32[64,128]{1,0:T(8,128)}, f32[64,128]{1,0:T(8,128)S(1)}, u32[]{:S(2)}) copy-start(f32[64,128]{1,0:T(8,128)S(1)} %fusion.34) | copy-start | bytes 98308
  4.2 4.4 %copy-start.1 = (bf16[64,64,64,1]{2,1,3,0:T(8,128)(2,1)S(1)}, bf16[64,64,64,1]{2,1,3,0:T(8,128)(2,1)}, u32[]{:S(2)}) copy-start(bf16[64,64,64,1]{2,1,3,0:T(8,128)(2,1)} %constant.186) | copy-start | bytes 1572868
  15.5 3.9 %copy-start.20 = (f32[16,2]{0,1:T(2,128)S(1)}, f32[16,2]{0,1:T(2,128)}, u32[]{:S(2)}) copy-start(f32[16,2]{0,1:T(2,128)} %param.14) | copy-start | bytes 388
  15.5 3.9 %copy-start.10 = (bf16[128,128,1,1]{1,0,2,3:T(8,128)(2,1)S(1)}, bf16[128,128,1,1]{1,0,2,3:T(8,128)(2,1)}, u32[]{:S(2)}) copy-start(bf16[128,128,1,1]{1,0,2,3:T(8,128)(2,1)} %constant.185) | copy-start | bytes 98308
  19.5 1.6 %copy-start.15 = (f32[16]{0:T(128)}, f32[16]{0:T(128)S(1)}, u32[]{:S(2)}) copy-start(f32[16]{0:T(128)S(1)} %get-tuple-element.42) | copy-start | bytes 196
  21.1 20.4 %copy-start.3 = (bf16[64,64,64]{2,1,0:T(8,128)(2,1)S(1)}, bf16[64,64,64]{2,1,0:T(8,128)(2,1)}, u32[]{:S(2)}) copy-start(bf16[64,64,64]{2,1,0:T(8,128)(2,1)} %constant.187) | copy-start | bytes 1572868
  23.8 21.2 %all-to-all-start = ((bf16[128,1,64]{2,1,0:T(2,128)(2,1)}), bf16[128,1,64]{2,1,0:T(2,128)(2,1)}, u32[]{:S(2)}, u32[]{:S(2)}) async-start(bf16[128,1,64]{2,1,0:T(2,128)(2,1)} %broadcast_in_dim.7), calls=%async_computation | async-start | bytes 131072 | tf_op jit(solution)/shard_map/all_to_all | solution.py:177
  39.8 2.1 %copy-start.13 = (bf16[2,64,128]{2,1,0:T(8,128)(2,1)S(1)}, bf16[2,64,128]{2,1,0:T(8,128)(2,1)}, u32[]{:S(2)}) copy-start(bf16[2,64,128]{2,1,0:T(8,128)(2,1)} %constant.188) | copy-start | bytes 98308
  41.5 1.9 %copy-start.11 = (s32[16,8]{0,1:T(8,128)S(1)}, s32[16,8]{0,1:T(8,128)}, u32[]{:S(2)}) copy-start(s32[16,8]{0,1:T(8,128)} %param.18) | copy-start | bytes 1540
  41.5 2.0 %copy-start.16 = (s32[16,8]{0,1:T(8,128)S(1)}, s32[16,8]{0,1:T(8,128)}, u32[]{:S(2)}) copy-start(s32[16,8]{0,1:T(8,128)} %param.19) | copy-start | bytes 1540
  41.5 2.6 %copy-start.17 = (f32[3,4]{1,0:T(4,128)S(1)}, f32[3,4]{1,0:T(4,128)}, u32[]{:S(2)}) copy-start(f32[3,4]{1,0:T(4,128)} %constant.122) | copy-start | bytes 148
  41.9 2.5 %copy-start.12 = (f32[3,16,8]{1,2,0:T(8,128)S(1)}, f32[3,16,8]{1,2,0:T(8,128)}, u32[]{:S(2)}) copy-start(f32[3,16,8]{1,2,0:T(8,128)} %param.17) | copy-start | bytes 4612
  42.2 29.4 %collective-permute-start = (bf16[16,64,128]{2,1,0:T(8,128)(2,1)S(1)}, bf16[16,64,128]{2,1,0:T(8,128)(2,1)S(1)}, u32[]{:S(2)}, u32[]{:S(2)}) collective-permute-start(bf16[16,64,128]{2,1,0:T(8,128)(2,1)S(1)} %get-tuple-element.43), channel_id=1, source_target_pairs={{0,16},{16,0},{32,48},{48,32},{64,80},{80,64},{96,112},{112,96},{1... | collective-permute-start | bytes 786440 | tf_op jit(solution)/shard_map/ppermute | solution.py:23
  43.3 4.8 %copy-start.14 = (f32[64]{0:T(128)S(1)}, f32[64]{0:T(128)}, u32[]{:S(2)}) copy-start(f32[64]{0:T(128)} %constant.112.clone) | copy-start | bytes 772
  48.8 23.0 %copy-start.9 = (bf16[128,128,1]{1,0,2:T(8,128)(2,1)S(1)}, bf16[128,128,1]{1,0,2:T(8,128)(2,1)}, u32[]{:S(2)}) copy-start(bf16[128,128,1]{1,0,2:T(8,128)(2,1)} %constant.189) | copy-start | bytes 98308
  71.6 1.4 %copy-start.2 = (bf16[64,64,64,1]{2,1,3,0:T(8,128)(2,1)S(1)}, bf16[64,64,64,1]{2,1,3,0:T(8,128)(2,1)}, u32[]{:S(2)}) copy-start(bf16[64,64,64,1]{2,1,3,0:T(8,128)(2,1)} %constant.186) | copy-start | bytes 1572868
  73.4 1.3 %copy-start.7 = (f32[64,128]{1,0:T(8,128)S(1)}, f32[64,128]{1,0:T(8,128)}, u32[]{:S(2)}) copy-start(f32[64,128]{1,0:T(8,128)} %copy-done.6) | copy-start | bytes 98308
  74.1 2.3 %copy-start.4 = (bf16[64,64,64]{2,1,0:T(8,128)(2,1)S(1)}, bf16[64,64,64]{2,1,0:T(8,128)(2,1)}, u32[]{:S(2)}) copy-start(bf16[64,64,64]{2,1,0:T(8,128)(2,1)} %constant.187) | copy-start | bytes 1572868
  74.7 1.9 %copy-start.5 = (f32[16,4,32,128]{3,2,1,0:T(8,128)S(1)}, f32[16,4,32,128]{3,2,1,0:T(8,128)}, u32[]{:S(2)}) copy-start(f32[16,4,32,128]{3,2,1,0:T(8,128)} %shard_map.139) | copy-start | bytes 3145732
  75.7 12.5 %copy-start.8 = (f32[64,64]{0,1:T(8,128)S(1)}, f32[64,64]{0,1:T(8,128)}, u32[]{:S(2)}) copy-start(f32[64,64]{0,1:T(8,128)} %fusion.33) | copy-start | bytes 49156
  78.4 19.4 %all-to-all-start.1 = ((f32[128,2,13]{2,1,0:T(2,128)}), f32[128,2,13]{2,1,0:T(2,128)S(1)}, u32[]{:S(2)}, u32[]{:S(2)}) async-start(f32[128,2,13]{2,1,0:T(2,128)} %bitcast.35), calls=%async_computation.1 | async-start | bytes 262144 | tf_op jit(solution)/shard_map/all_to_all | solution.py:227
